TPU v7x, 256 devices: a whole 4x4x8 slice. The times are simulated.
256 devices in a mesh: gx: 8 (over y, core), gy: 4 (over z_hi), gz: 8 (over x, z_lo).
Axes of the slice: x: 4, y: 4, z: 8 (z_hi: 4, z_lo: 2; z = z_hi * 2 + z_lo), core: 2. Of those that a mesh axis runs over, the one named last changes fastest.
Arguments:
- scalars: float32 [8, 4, 8, 128, 128], P('gx', 'gy', 'gz'), may hold values from -6 to 6
- vectors: float32 [8, 4, 8, 3, 128, 128], P('gx', 'gy', 'gz'), may hold values from -6 to 6
- positions: float32 [8, 4, 8, 3, 128], P('gx', 'gy', 'gz'), may hold values from 0 to 6
- species: int32 [8, 4, 8, 128], P('gx', 'gy', 'gz'), may hold values from 0 to 7
- atom_count: int32 [8, 4, 8], P('gx', 'gy', 'gz'), may hold values from 64 to 128, as said below
- energy_weight: float32 [8, 4, 8, 128], P('gx', 'gy', 'gz'), may hold values from -5 to 5
- local_pairs: int32 [8, 4, 8, 2, 1024], P('gx', 'gy', 'gz'), may hold values from 0 to 127, as said below
- face_pairs: int32 [8, 4, 8, 3, 2, 256], P('gx', 'gy', 'gz'), may hold values from 0 to 127, as said below
- tile_counts: int32 [8, 4, 8, 4], P('gx', 'gy', 'gz'), may hold values from 85 to 1024, as said below
- w_center: float32 [128, 128], replicated, may hold values from -0.5 to 0.5
- w_partner: float32 [128, 128], replicated, may hold values from -0.5 to 0.5
- w_radial: float32 [8, 128], replicated, may hold values from -4 to 4
- species_embed: float32 [2, 8, 128], replicated, may hold values from -3 to 3
- w_mix: float32 [128, 128], replicated, may hold values from -0.5 to 0.5
- w_channel: float32 [2, 128, 128], replicated, may hold values from -0.5 to 0.5
- w_read: float32 [128, 128], replicated, may hold values from -0.5 to 0.5
- w_out: float32 [128], replicated, may hold values from -0.5 to 0.5
- species_energy: float32 [8], replicated, may hold values from -2 to 2
Outputs:
- atom_energy: float32 [8, 4, 8, 128], P('gx', 'gy', 'gz')
- position_grad: float32 [8, 4, 8, 3, 128], P('gx', 'gy', 'gz')
- scalar_grad: float32 [8, 4, 8, 128, 128], P('gx', 'gy', 'gz')
- vector_grad: float32 [8, 4, 8, 3, 128, 128], P('gx', 'gy', 'gz')
- weight_grad: float32 [101512], replicated
Inputs may be any that keep to these rules, and one draw needn't show every extreme that they name: `atom_count`: some domain holds exactly 128 live atoms; slots at or above a domain's count are padding. `tile_counts`: entry 0 counts the live slots of the local tile (at least 512), entries 1 to 3 those of the face tiles (at least 85); some domain fills all four tiles. `local_pairs`: every slot names two different atoms of the domain, both below its atom count; live slots are those below tile_counts[0]. `face_pairs`: in tile d, entry 0 names an atom below this domain's count and entry 1 an atom below the count of the next domain along grid direction d (wrapping around); live slots are those below tile_counts[1 + d].
All inputs are finite; a program needn't handle non-finite values.
Results may differ from a plain program's by a relative error of at most 0.0003.
Values sent between devices are 32-bit elements; how exact they have to be, the bound alone decides.
No kernel may reach another device: no remote copies, remote signals or barrier semaphores. Data moves between devices by JAX's collectives and lax.ppermute only.
A program may use at most 128 MiB of HBM per device.

v0:
```python
import jax
import jax.numpy as jnp
from jax import lax
from jax.sharding import PartitionSpec as P

cutoff_radius = 5.0
cell_edge = 6.0
highest = lax.Precision.HIGHEST
halving_count = 3


def from_behind(block, axis, distance):
    devices = range(lax.axis_size(axis))
    route = [((i - distance) % len(devices), i) for i in devices]
    return lax.ppermute(block, axis, route)


def edge_energy(edge_params, center_proj, partner_proj, center_vecs, partner_vecs, displace):
    radial_weight, mix_weight, channel_weight, read_weight, out_weight = edge_params
    squared = jnp.sum(displace * displace, axis=0)
    basis_count = radial_weight.shape[0]
    spacing = cutoff_radius * cutoff_radius / (basis_count - 1)
    centers_sq = spacing * jnp.arange(basis_count).astype(jnp.float32)
    radial_basis = jnp.exp(-jnp.square((squared[None, :] - centers_sq[:, None]) / spacing))
    latent_in = (
        center_proj + partner_proj + jnp.dot(radial_weight.T, radial_basis, precision=lax.Precision.HIGH)
    )
    first_hidden = jax.nn.silu(latent_in)
    second = first_hidden + jax.nn.silu(jnp.dot(mix_weight.T, first_hidden, precision=lax.Precision.HIGH))
    vector_gain = jnp.dot(channel_weight[0].T, second, precision=lax.Precision.HIGH)
    tensor_gain = jnp.dot(channel_weight[1].T, second, precision=lax.Precision.HIGH)
    bond_vector = displace / cutoff_radius
    along_partner = jnp.sum(bond_vector[:, None, :] * partner_vecs, axis=0)
    along_center = jnp.sum(bond_vector[:, None, :] * center_vecs, axis=0)
    inner_product = jnp.sum(center_vecs * partner_vecs, axis=0)
    scaled_sq = squared / (cutoff_radius * cutoff_radius)
    quadratic = along_center * along_partner - scaled_sq[None, :] * inner_product / 3.0
    mixed_latent = second + vector_gain * along_partner + tensor_gain * quadratic
    readout = jnp.dot(
        out_weight,
        jax.nn.silu(jnp.dot(read_weight.T, mixed_latent, precision=lax.Precision.HIGH)),
        precision=highest,
    )
    envelope = 1.0 / (1.0 + scaled_sq)
    return envelope * readout


def shift(payload, direction, distance):
    return from_behind(payload, ("gx", "gy", "gz")[direction], distance)


def halving_steps():
    steps = []
    for axis in ("gx", "gz", "gy"):
        size = lax.axis_size(axis)
        distance = 1
        while distance < size:
            steps.append((axis, distance, size))
            distance *= 2
    return steps


def sum_over_devices(rows):
    steps = halving_steps()
    if any(size & (size - 1) for _, _, size in steps):
        return lax.psum(rows, ("gx", "gy", "gz"))
    halvings = min(halving_count, len(steps))
    padded = jnp.pad(rows, ((0, (-rows.shape[0]) % (2**halvings)), (0, 0)))
    for axis, distance, size in steps[:halvings]:
        upper = (lax.axis_index(axis) // distance) % 2 == 1
        half = padded.shape[0] // 2
        low, high = padded[:half], padded[half:]
        keep = jnp.where(upper, high, low)
        send = jnp.where(upper, low, high)
        padded = keep + lax.ppermute(send, axis, [(i, i ^ distance) for i in range(size)])
    for axis, distance, size in steps[halvings:]:
        padded = padded + lax.ppermute(padded, axis, [(i, i ^ distance) for i in range(size)])
    for axis, distance, size in reversed(steps[:halvings]):
        upper = (lax.axis_index(axis) // distance) % 2 == 1
        other = lax.ppermute(padded, axis, [(i, i ^ distance) for i in range(size)])
        padded = jnp.where(
            upper, jnp.concatenate([other, padded]), jnp.concatenate([padded, other])
        )
    return padded[: rows.shape[0]]


def one_hot(rows, slots):
    return (jnp.arange(slots, dtype=jnp.int32)[:, None] == rows[None, :]).astype(jnp.float32)


def per_device(
    scalars,
    vectors,
    positions,
    species,
    atom_count,
    energy_weight,
    local_pairs,
    face_pairs,
    tile_counts,
    w_center,
    w_partner,
    w_radial,
    species_embed,
    w_mix,
    w_channel,
    w_read,
    w_out,
    species_energy,
):
    scalar_in = scalars[0, 0, 0]
    vector_in = vectors[0, 0, 0]
    coords = positions[0, 0, 0]
    weights_here = energy_weight[0, 0, 0]
    live_counts = tile_counts[0, 0, 0]
    local_list = local_pairs[0, 0, 0]
    face_list = face_pairs[0, 0, 0]
    channels, atom_slots = scalar_in.shape
    vector_rows = 3 * channels
    table_rows = channels + vector_rows + 3
    kind_count = species_energy.shape[0]
    local_slots = local_list.shape[1]
    face_slots = face_list.shape[2]
    species_hot = (
        species[0, 0, 0][None, :] == jnp.arange(kind_count, dtype=jnp.int32)[:, None]
    ).astype(jnp.float32)
    valid_atoms = (jnp.arange(atom_slots, dtype=jnp.int32) < atom_count[0, 0, 0]).astype(
        jnp.float32
    )

    edge_params = (w_radial, w_mix, w_channel, w_read, w_out)
    vector_flat = vector_in.reshape(vector_rows, atom_slots)
    own_table = jnp.concatenate([scalar_in, vector_flat, coords], axis=0)
    species_row = species[0, 0, 0].astype(jnp.float32)
    packet = jnp.concatenate([own_table, weights_here[None, :], species_row[None, :]], axis=0)
    arrived = [shift(packet, direction, -1) for direction in range(3)]
    far_tables = [incoming[:table_rows] for incoming in arrived]
    partner_weights = [weights_here] + [incoming[table_rows] for incoming in arrived]
    partner_species = [species_hot] + [
        (incoming[table_rows + 1][None, :] == jnp.arange(kind_count, dtype=jnp.float32)[:, None]).astype(
            jnp.float32
        )
        for incoming in arrived
    ]

    center_rows = jnp.concatenate([local_list[0]] + [face_list[d, 0] for d in range(3)])
    partner_rows = [local_list[1]] + [face_list[d, 1] for d in range(3)]
    center_hot = one_hot(center_rows, atom_slots)
    partner_hot = [one_hot(rows, atom_slots) for rows in partner_rows]
    slot_sizes = [local_slots] + [face_slots] * 3
    live_mask = jnp.concatenate(
        [
            (jnp.arange(size, dtype=jnp.int32) < live_counts[tile]).astype(jnp.float32)
            for tile, size in enumerate(slot_sizes)
        ]
    )
    offset = jnp.concatenate(
        [jnp.zeros((3, local_slots), jnp.float32)]
        + [
            jnp.broadcast_to(
                cell_edge * (jnp.arange(3) == d).astype(jnp.float32)[:, None], (3, face_slots)
            )
            for d in range(3)
        ],
        axis=1,
    )
    pair_weight = jnp.dot(weights_here, center_hot, precision=lax.Precision.HIGH) + jnp.concatenate(
        [
            jnp.dot(weight_row, hot, precision=lax.Precision.HIGH)
            for weight_row, hot in zip(partner_weights, partner_hot)
        ]
    )

    def pair_loss(center_matrix, partner_matrix, embed_table, params_in, own_in, far_in):
        def projected(matrix, embed_row, table, hot_kinds):
            proj = jnp.dot(matrix.T, table[:channels], precision=lax.Precision.HIGH) + jnp.dot(
                embed_row.T, hot_kinds, precision=highest
            )
            return jnp.concatenate([proj, table[channels:]], axis=0)

        center_in = projected(center_matrix, embed_table[0], own_in, species_hot)
        partner_in = [
            projected(partner_matrix, embed_table[1], table, hot_kinds)
            for table, hot_kinds in zip([own_in] + list(far_in), partner_species)
        ]
        center_side = jnp.dot(center_in, center_hot, precision=lax.Precision.HIGH)
        partner_side = jnp.concatenate(
            [jnp.dot(table, hot, precision=lax.Precision.HIGH) for table, hot in zip(partner_in, partner_hot)],
            axis=1,
        )
        pair_count = center_side.shape[1]
        displace = (
            partner_side[channels + vector_rows :] + offset - center_side[channels + vector_rows :]
        )
        energies = edge_energy(
            params_in,
            center_side[:channels],
            partner_side[:channels],
            center_side[channels : channels + vector_rows].reshape(3, channels, pair_count),
            partner_side[channels : channels + vector_rows].reshape(3, channels, pair_count),
            displace,
        )
        halves = 0.5 * live_mask * energies
        return jnp.sum(halves * pair_weight), halves

    weighted_sum, pull_back, halves = jax.vjp(
        pair_loss, w_center, w_partner, species_embed, edge_params, own_table, far_tables,
        has_aux=True,
    )
    center_matrix_grad, partner_matrix_grad, embed_grad, param_grad, own_grad, far_grad = pull_back(
        jnp.ones_like(weighted_sum)
    )
    center_energy = jnp.dot(center_hot, halves, precision=lax.Precision.HIGH)
    starts = [0, local_slots] + [local_slots + face_slots * (d + 1) for d in range(3)]
    partner_energy = [
        jnp.dot(hot, halves[starts[tile] : starts[tile + 1]], precision=lax.Precision.HIGH)
        for tile, hot in enumerate(partner_hot)
    ]

    returned = [
        shift(jnp.concatenate([far_grad[d], partner_energy[d + 1][None, :]], axis=0), d, 1)
        for d in range(3)
    ]
    table_grad = own_grad
    for back_in in returned:
        table_grad = table_grad + back_in[:table_rows]
    pair_energy = center_energy + partner_energy[0]
    for back_in in returned:
        pair_energy = pair_energy + back_in[table_rows]
    scalar_grad = table_grad[:channels]
    vector_grad = table_grad[channels : channels + vector_rows].reshape(3, channels, atom_slots)
    coord_grad = table_grad[channels + vector_rows :]

    self_energy = valid_atoms * jnp.dot(species_energy, species_hot, precision=lax.Precision.HIGH)
    reference_grad = jnp.dot(species_hot, weights_here * valid_atoms, precision=lax.Precision.HIGH)
    lanes = channels

    def as_rows(piece):
        flat = piece.reshape(-1)
        return jnp.pad(flat, (0, (-flat.shape[0]) % lanes)).reshape(-1, lanes)

    grad_pieces = [
        center_matrix_grad,
        partner_matrix_grad,
        param_grad[0],
        embed_grad,
        param_grad[1],
        param_grad[2],
        param_grad[3],
    ]
    tail = jnp.concatenate([param_grad[4].reshape(-1), reference_grad])
    sizes = [piece.size for piece in grad_pieces] + [tail.shape[0]]
    local_rows = jnp.concatenate([as_rows(piece) for piece in grad_pieces] + [as_rows(tail)], axis=0)
    domain_total = lax.axis_size("gx") * lax.axis_size("gy") * lax.axis_size("gz")
    summed = sum_over_devices(local_rows) / domain_total
    weight_grad = summed.reshape(-1)[: sum(sizes)]
    atom_energy = self_energy + pair_energy
    return (
        atom_energy[None, None, None],
        coord_grad[None, None, None],
        scalar_grad[None, None, None],
        vector_grad[None, None, None],
        weight_grad,
    )


def solution(mesh):
    return jax.shard_map(
        per_device,
        mesh=mesh,
        in_specs=(
            P("gx", "gy", "gz", None, None),
            P("gx", "gy", "gz", None, None, None),
            P("gx", "gy", "gz", None, None),
            P("gx", "gy", "gz", None),
            P("gx", "gy", "gz"),
            P("gx", "gy", "gz", None),
            P("gx", "gy", "gz", None, None),
            P("gx", "gy", "gz", None, None, None),
            P("gx", "gy", "gz", None),
            P(),
            P(),
            P(),
            P(),
            P(),
            P(),
            P(),
            P(),
            P(),
        ),
        out_specs=(
            P("gx", "gy", "gz", None),
            P("gx", "gy", "gz", None, None),
            P("gx", "gy", "gz", None, None),
            P("gx", "gy", "gz", None, None, None),
            P(),
        ),
        check_vma=False,
    )
```

profile of v0, /device:TPU:15, one launch (start us, length us, event | category | flops | bytes accessed | tf_op | source)
XLA Modules:
  0.0 123.0 jit_solution(17321030975140355810)
XLA Ops:
  2.0 2.5 %concatenate.78 = f32[517,128]{1,0:T(8,128)S(1)} concatenate(f32[128,128]{1,0:T(8,128)} %bitcast.316, f32[384,128]{1,0:T(8,128)} %bitcast.313, f32[3,128]{1,0:T(4,128)S(1)} %bitcast.324, f32[1,128]{1,0:T(1,128)} %bitcast.362, f32[1,128]{1,0:T(1,128)S(1)} %convert_bitcast_fusion), dimensions={0} | concatenate | bytes 529408 | tf_op jit(solution)/shard_map/concatenate | solution.py:135
  4.5 1.9 %collective-permute-start.2 = (f32[517,128]{1,0:T(8,128)S(1)}, f32[517,128]{1,0:T(8,128)S(1)}, u32[]{:S(2)}, u32[]{:S(2)}) collective-permute-start(f32[517,128]{1,0:T(8,128)S(1)} %concatenate.78), channel_id=1, source_target_pairs={{1,0},{2,1},{3,2},{4,3},{5,4},{6,5},{7,6},{0,7},{9,8},{10,9},{11,1... | collective-permute-start | bytes 794120 | tf_op jit(solution)/shard_map/ppermute | solution.py:15
  6.4 5.1 %collective-permute-start.1 = (f32[517,128]{1,0:T(8,128)S(1)}, f32[517,128]{1,0:T(8,128)S(1)}, u32[]{:S(2)}, u32[]{:S(2)}) collective-permute-start(f32[517,128]{1,0:T(8,128)S(1)} %concatenate.78), channel_id=1, source_target_pairs={{8,0},{16,8},{24,16},{0,24},{9,1},{17,9},{25,17},{1,25},{10,2},{18... | collective-permute-start | bytes 794120 | tf_op jit(solution)/shard_map/ppermute | solution.py:15
  11.5 1.2 %collective-permute-start = (f32[517,128]{1,0:T(8,128)S(1)}, f32[517,128]{1,0:T(8,128)S(1)}, u32[]{:S(2)}, u32[]{:S(2)}) collective-permute-start(f32[517,128]{1,0:T(8,128)S(1)} %concatenate.78), channel_id=1, source_target_pairs={{32,0},{64,32},{96,64},{128,96},{160,128},{192,160},{224,192},{0,2... | collective-permute-start | bytes 794120 | tf_op jit(solution)/shard_map/ppermute | solution.py:15
  13.4 1.4 %fusion.210 = (s32[1,1,1,1]{3,2,1,0:T(1,128)}, s32[1,1,1,1]{3,2,1,0:T(1,128)}, s32[1,1,1,1]{3,2,1,0:T(1,128)}, s32[1,1,1,1]{3,2,1,0:T(1,128)}) fusion(s32[1,1,1,4]{3,2,1,0:T(1,128)} %param.26), kind=kLoop, calls=%fused_computation.348 | loop fusion | bytes 32 | tf_op jit(solution)/shard_map/slice | solution.py:153
  16.2 0.8 fusion.209
  17.0 0.8 fusion.208
  17.8 0.9 fusion.43
  18.7 1.0 convolution_reduce_fusion
  19.7 1.1 fusion.189
  20.8 1.1 fusion.191
  21.9 1.4 %convolution_bitcast_fusion.28 = f32[8]{0:T(128)} fusion(s32[128]{0:T(128)} %bitcast.342, f32[1,1,1,128]{3,2,1,0:T(1,128)} %param.23, s32[]{:T(128)} %bitcast.308), kind=kOutput, calls=%fused_computation.78 | convolution fusion | flops 7424 | bytes 1060 | tf_op jit(solution)/shard_map/dot_general | solution.py:235
  23.3 1.0 fusion.18
  24.2 1.0 fusion.19
  25.2 2.1 %fusion.36 = f32[515,1792]{1,0:T(8,128)S(1)} fusion(s32[1792]{0:T(1024)S(1)} %pad_add_fusion.6, f32[3,128]{1,0:T(4,128)S(1)} %bitcast.325, f32[384,128]{1,0:T(8,128)} %bitcast.314, f32[128,128]{1,0:T(8,128)S(1)} %fusion.18), kind=kOutput, calls=%fused_computation.102 | convolution fusion | flops 709133056 | bytes 3962368 | tf_op jit(solution)/shard_map/jvp()/dot_general | solution.py:186
  27.5 1.3 %iota_compare_fusion.42 = (pred[256]{0:T(512)(128)(4,1)S(1)}, pred[256]{0:T(512)(128)(4,1)S(1)}) fusion(s32[]{:T(128)} %bitcast.12, s32[]{:T(128)} %bitcast.11), kind=kLoop, calls=%fused_computation.298 | loop fusion | flops 512 | bytes 520 | tf_op jit(solution)/shard_map/lt | solution.py:153
  34.9 1.0 multiply_add_fusion.2
  37.2 0.9 multiply_add_fusion.1
  38.6 0.8 convolution_reduce_fusion.1
  39.4 1.2 %negate_multiply_fusion = (f32[128,1792]{1,0:T(8,128)S(1)}, f32[128,1792]{1,0:T(8,128)S(1)}, f32[128,1792]{1,0:T(8,128)S(1)}, f32[1792]{0:T(1024)S(1)}, f32[128,1792]{1,0:T(8,128)S(1)}) fusion(f32[1792]{0:T(1024)S(1)} %get-tuple-element.44, f32[128,1792]{1,0:T(8,128)S(1)} %get-tuple-element.63, f32[128,1792]{1,0:T(8,128)S(1)} %get-tuple-element.12, ...), kind=kOutput, calls=%fused_computation.103 | convolution fusion | flops 180746496 | bytes 9262592 | tf_op jit(solution)/shard_map/transpose(jvp())/dot_general | solution.py:41
  41.3 1.4 %convolution_bitcast_fusion.13 = f32[1,128,128]{2,1,0:T(8,128)} fusion(f32[128,1792]{1,0:T(8,128)S(1)} %get-tuple-element.61, f32[128,1792]{1,0:T(8,128)S(1)} %get-tuple-element.64, f32[128,1792]{1,0:T(8,128)S(1)} %get-tuple-element.16), kind=kOutput, calls=%fused_computation.50 | convolution fusion | flops 176390144 | bytes 2818048 | tf_op jit(solution)/shard_map/transpose(jvp())/dot_general | solution.py:31
  43.8 1.1 fusion.33
  45.3 1.3 %broadcast_multiply_fusion = (f32[3,128,1792]{2,1,0:T(8,128)S(1)}, f32[3,1792]{1,0:T(4,128)}, f32[3,1792]{1,0:T(4,128)}, f32[3,128,1792]{2,1,0:T(8,128)S(1)}) fusion(f32[128,1792]{1,0:T(8,128)S(1)} %get-tuple-element.21, f32[3,1792]{1,0:T(4,128)S(1)} %get-tuple-element.17, f32[3,128,1792]{2,1,0:T(8,128)S(1)} %bitcast.312, f32[3,128,1792]{2,1,0:T(8,128)S(1)} %bitcast.310, ...), kind=kLoop, calls=%fused_computation.39 | loop fusion | flops 4118016 | bytes 12909568 | tf_op jit(solution)/shard_map/transpose(jvp())/mul | solution.py:34
  47.2 2.5 %fusion.7 = (f32[384,1792]{1,0:T(8,128)}, f32[384,1792]{1,0:T(8,128)S(1)}) fusion(f32[384,1792]{1,0:T(8,128)S(1)} %pad_maximum_fusion, f32[3,128,1792]{2,1,0:T(8,128)S(1)} %get-tuple-element.25, f32[128,1792]{1,0:T(8,128)S(1)} %get-tuple-element.19, f32[3,128,1792]{2,1,0:T(8,128)S(1)} %get-tuple-element.36, f32[515,1792]{1,0:T(8,128)S(1)} %fusion.36), kind=kLoop, calls=%fused_computation.10 | loop fusion | flops 2752512 | bytes 17432576 | tf_op jit(solution)/shard_map/transpose(jvp())/add_any | solution.py:34
  49.7 0.8 fusion.206
  50.6 3.0 %fusion.2 = f32[515,128]{1,0:T(8,128)S(1)} fusion(f32[128,1792]{1,0:T(8,128)S(1)} %fusion.33, f32[3,1792]{1,0:T(4,128)S(1)} %get-tuple-element.13, f32[384,1792]{1,0:T(8,128)} %get-tuple-element.23, s32[1792]{0:T(1024)} %copy-done.15), kind=kOutput, calls=%fused_computation.6 | convolution fusion | flops 710846976 | bytes 3962368 | tf_op jit(solution)/shard_map/transpose(jvp())/dot_general | solution.py:186
  58.1 0.9 convolution_bitcast_fusion.26
  59.3 1.0 fusion.103
  61.4 1.0 constant_dynamic-update-slice_fusion.2
  62.5 0.9 convolution_dynamic-update-slice_fusion
  64.1 0.9 collective-permute-done.6
  65.0 1.8 %collective-permute-start.7 = (f32[200,128]{1,0:T(8,128)S(1)}, f32[200,128]{1,0:T(8,128)S(1)}, u32[]{:S(2)}, u32[]{:S(2)}) collective-permute-start(f32[200,128]{1,0:T(8,128)S(1)} %slice_select_fusion.1), channel_id=1, source_target_pairs={{0,64},{32,96},{64,0},{96,32},{128,192},{160,224},{192,128},{224,1... | collective-permute-start | bytes 307208 | tf_op jit(solution)/shard_map/ppermute | solution.py:75
  66.8 2.9 %collective-permute-done.7 = f32[200,128]{1,0:T(8,128)S(1)} collective-permute-done((f32[200,128]{1,0:T(8,128)S(1)}, f32[200,128]{1,0:T(8,128)S(1)}, u32[]{:S(2)}, u32[]{:S(2)}) %collective-permute-start.7) | collective-permute-done | bytes 102432 | tf_op jit(solution)/shard_map/ppermute | solution.py:75
  69.7 1.8 %collective-permute-start.8 = (f32[100,128]{1,0:T(8,128)S(1)}, f32[100,128]{1,0:T(8,128)S(1)}, u32[]{:S(2)}, u32[]{:S(2)}) collective-permute-start(f32[100,128]{1,0:T(8,128)S(1)} %slice_select_fusion.2), channel_id=1, source_target_pairs={{0,128},{32,160},{64,192},{96,224},{128,0},{160,32},{192,64},{224,... | collective-permute-start | bytes 153608 | tf_op jit(solution)/shard_map/ppermute | solution.py:75
  71.6 2.0 %collective-permute-start.3 = (f32[516,128]{1,0:T(8,128)S(1)}, f32[516,128]{1,0:T(8,128)S(1)}, u32[]{:S(2)}, u32[]{:S(2)}) collective-permute-start(f32[516,128]{1,0:T(8,128)S(1)} %pad_maximum_fusion.11), channel_id=1, source_target_pairs={{224,0},{0,32},{32,64},{64,96},{96,128},{128,160},{160,192},{192,2... | collective-permute-start | bytes 792584 | tf_op jit(solution)/shard_map/ppermute | solution.py:15
  73.6 1.0 collective-permute-done.8
  75.1 4.2 %collective-permute-done.9 = f32[100,128]{1,0:T(8,128)S(1)} collective-permute-done((f32[100,128]{1,0:T(8,128)S(1)}, f32[100,128]{1,0:T(8,128)S(1)}, u32[]{:S(2)}, u32[]{:S(2)}) %collective-permute-start.9) | collective-permute-done | bytes 51232 | tf_op jit(solution)/shard_map/ppermute | solution.py:77
  79.9 2.4 %collective-permute-start.5 = (f32[516,128]{1,0:T(8,128)S(1)}, f32[516,128]{1,0:T(8,128)S(1)}, u32[]{:S(2)}, u32[]{:S(2)}) collective-permute-start(f32[516,128]{1,0:T(8,128)S(1)} %pad_maximum_fusion.13), channel_id=1, source_target_pairs={{7,0},{0,1},{1,2},{2,3},{3,4},{4,5},{5,6},{6,7},{15,8},{8,9},{9,10... | collective-permute-start | bytes 792584 | tf_op jit(solution)/shard_map/ppermute | solution.py:15
  82.3 1.2 collective-permute-start.11
  83.7 3.1 %collective-permute-done.11 = f32[100,128]{1,0:T(8,128)S(1)} collective-permute-done((f32[100,128]{1,0:T(8,128)S(1)}, f32[100,128]{1,0:T(8,128)S(1)}, u32[]{:S(2)}, u32[]{:S(2)}) %collective-permute-start.11) | collective-permute-done | bytes 51232 | tf_op jit(solution)/shard_map/ppermute | solution.py:77
  87.4 3.5 %collective-permute-done.12 = f32[100,128]{1,0:T(8,128)S(1)} collective-permute-done((f32[100,128]{1,0:T(8,128)S(1)}, f32[100,128]{1,0:T(8,128)S(1)}, u32[]{:S(2)}, u32[]{:S(2)}) %collective-permute-start.12) | collective-permute-done | bytes 51232 | tf_op jit(solution)/shard_map/ppermute | solution.py:77
  90.9 1.9 %collective-permute-start.13 = (f32[100,128]{1,0:T(8,128)S(1)}, f32[100,128]{1,0:T(8,128)S(1)}, u32[]{:S(2)}, u32[]{:S(2)}) collective-permute-start(f32[100,128]{1,0:T(8,128)S(1)} %add.206), channel_id=1, source_target_pairs={{0,16},{8,24},{16,0},{24,8},{1,17},{9,25},{17,1},{25,9},{2,18},{10... | collective-permute-start | bytes 153608 | tf_op jit(solution)/shard_map/ppermute | solution.py:77
  92.9 4.9 %collective-permute-done.13 = f32[100,128]{1,0:T(8,128)S(1)} collective-permute-done((f32[100,128]{1,0:T(8,128)S(1)}, f32[100,128]{1,0:T(8,128)S(1)}, u32[]{:S(2)}, u32[]{:S(2)}) %collective-permute-start.13) | collective-permute-done | bytes 51232 | tf_op jit(solution)/shard_map/ppermute | solution.py:77
  97.8 2.5 %collective-permute-start.14 = (f32[100,128]{1,0:T(8,128)S(1)}, f32[100,128]{1,0:T(8,128)S(1)}, u32[]{:S(2)}, u32[]{:S(2)}) collective-permute-start(f32[100,128]{1,0:T(8,128)S(1)} %add.207), channel_id=1, source_target_pairs={{0,128},{32,160},{64,192},{96,224},{128,0},{160,32},{192,64},{224,... | collective-permute-start | bytes 153608 | tf_op jit(solution)/shard_map/ppermute | solution.py:80
  101.6 0.8 collective-permute-done.14
  103.3 2.7 %collective-permute-done.15 = f32[200,128]{1,0:T(8,128)S(1)} collective-permute-done((f32[200,128]{1,0:T(8,128)S(1)}, f32[200,128]{1,0:T(8,128)S(1)}, u32[]{:S(2)}, u32[]{:S(2)}) %collective-permute-start.15) | collective-permute-done | bytes 102432 | tf_op jit(solution)/shard_map/ppermute | solution.py:80
  106.1 15.1 %collective-permute-start.16 = (f32[400,128]{1,0:T(8,128)S(1)}, f32[400,128]{1,0:T(8,128)S(1)}, u32[]{:S(2)}, u32[]{:S(2)}) collective-permute-start(f32[400,128]{1,0:T(8,128)S(1)} %maximum_select_fusion), channel_id=1, source_target_pairs={{0,32},{32,0},{64,96},{96,64},{128,160},{160,128},{192,224},{224,1... | collective-permute-start | bytes 614408 | tf_op jit(solution)/shard_map/ppermute | solution.py:80
  122.2 0.8 fusion.51
  (209 shorter events, 24.8 us)
Async XLA Ops:
  0.6 37.4 %copy-start = (f32[128,128]{1,0:T(8,128)S(1)}, f32[128,128]{1,0:T(8,128)}, u32[]{:S(2)}) copy-start(f32[128,128]{1,0:T(8,128)} %param.33) | copy-start | bytes 196612
  4.5 25.2 %collective-permute-start.2 = (f32[517,128]{1,0:T(8,128)S(1)}, f32[517,128]{1,0:T(8,128)S(1)}, u32[]{:S(2)}, u32[]{:S(2)}) collective-permute-start(f32[517,128]{1,0:T(8,128)S(1)} %concatenate.78), channel_id=1, source_target_pairs={{1,0},{2,1},{3,2},{4,3},{5,4},{6,5},{7,6},{0,7},{9,8},{10,9},{11,1... | collective-permute-start | bytes 794120 | tf_op jit(solution)/shard_map/ppermute | solution.py:15
  6.4 23.8 %collective-permute-start.1 = (f32[517,128]{1,0:T(8,128)S(1)}, f32[517,128]{1,0:T(8,128)S(1)}, u32[]{:S(2)}, u32[]{:S(2)}) collective-permute-start(f32[517,128]{1,0:T(8,128)S(1)} %concatenate.78), channel_id=1, source_target_pairs={{8,0},{16,8},{24,16},{0,24},{9,1},{17,9},{25,17},{1,25},{10,2},{18... | collective-permute-start | bytes 794120 | tf_op jit(solution)/shard_map/ppermute | solution.py:15
  11.5 18.9 %collective-permute-start = (f32[517,128]{1,0:T(8,128)S(1)}, f32[517,128]{1,0:T(8,128)S(1)}, u32[]{:S(2)}, u32[]{:S(2)}) collective-permute-start(f32[517,128]{1,0:T(8,128)S(1)} %concatenate.78), channel_id=1, source_target_pairs={{32,0},{64,32},{96,64},{128,96},{160,128},{192,160},{224,192},{0,2... | collective-permute-start | bytes 794120 | tf_op jit(solution)/shard_map/ppermute | solution.py:15
  12.7 32.2 %copy-start.26 = (f32[8]{0:T(128)}, f32[8]{0:T(128)S(1)}, u32[]{:S(2)}) copy-start(f32[8]{0:T(128)S(1)} %convert_multiply_fusion) | copy-start | bytes 100
  16.9 16.1 %copy-start.18 = (s32[1,1,256]{2,1,0:T(1,128)}, s32[1,1,256]{2,1,0:T(1,128)S(1)}, u32[]{:S(2)}) copy-start(s32[1,1,256]{2,1,0:T(1,128)S(1)} %get-tuple-element.50) | copy-start | bytes 3076
  16.9 16.2 %copy-start.20 = (s32[1,1,256]{2,1,0:T(1,128)}, s32[1,1,256]{2,1,0:T(1,128)S(1)}, u32[]{:S(2)}) copy-start(s32[1,1,256]{2,1,0:T(1,128)S(1)} %get-tuple-element.51) | copy-start | bytes 3076
  17.0 16.3 %copy-start.22 = (s32[1,1,256]{2,1,0:T(1,128)}, s32[1,1,256]{2,1,0:T(1,128)S(1)}, u32[]{:S(2)}) copy-start(s32[1,1,256]{2,1,0:T(1,128)S(1)} %get-tuple-element.52) | copy-start | bytes 3076
  18.7 8.9 %copy-start.15 = (s32[1792]{0:T(1024)}, s32[1792]{0:T(1024)S(1)}, u32[]{:S(2)}) copy-start(s32[1792]{0:T(1024)S(1)} %pad_add_fusion.6) | copy-start | bytes 21508
  27.3 2.3 %copy-start.14 = (f32[2,8,128]{2,1,0:T(8,128)S(1)}, f32[2,8,128]{2,1,0:T(8,128)}, u32[]{:S(2)}) copy-start(f32[2,8,128]{2,1,0:T(8,128)} %param.30) | copy-start | bytes 24580
  27.5 3.3 %copy-start.1 = (f32[128,128]{1,0:T(8,128)S(1)}, f32[128,128]{1,0:T(8,128)}, u32[]{:S(2)}) copy-start(f32[128,128]{1,0:T(8,128)} %param.28) | copy-start | bytes 196612
  30.2 2.5 %copy-start.28 = (f32[128]{0:T(128)}, f32[128]{0:T(128)S(1)}, u32[]{:S(2)}) copy-start(f32[128]{0:T(128)S(1)} %slice_bitcast_fusion.12) | copy-start | bytes 1540
  30.5 2.9 %copy-start.8 = (f32[517,128]{1,0:T(8,128)}, f32[517,128]{1,0:T(8,128)S(1)}, u32[]{:S(2)}) copy-start(f32[517,128]{1,0:T(8,128)S(1)} %collective-permute-done) | copy-start | bytes 794116
  30.5 2.0 %copy-start.32 = (f32[128]{0:T(128)}, f32[128]{0:T(128)S(1)}, u32[]{:S(2)}) copy-start(f32[128]{0:T(128)S(1)} %slice_bitcast_fusion.13) | copy-start | bytes 1540
  33.5 6.0 %copy-start.11 = (f32[1792]{0:T(1024)}, f32[1792]{0:T(1024)S(1)}, u32[]{:S(2)}) copy-start(f32[1792]{0:T(1024)S(1)} %get-tuple-element.45) | copy-start | bytes 21508
  35.9 7.9 %copy-start.39 = (f32[128,1792]{1,0:T(8,128)}, f32[128,1792]{1,0:T(8,128)S(1)}, u32[]{:S(2)}) copy-start(f32[128,1792]{1,0:T(8,128)S(1)} %get-tuple-element.62) | copy-start | bytes 2752516
  50.5 3.0 %copy-start.24 = (s32[1,1,1,128]{3,2,1,0:T(1,128)S(1)}, s32[1,1,1,128]{3,2,1,0:T(1,128)}, u32[]{:S(2)}) copy-start(s32[1,1,1,128]{3,2,1,0:T(1,128)} %param.21) | copy-start | bytes 1540
  50.6 3.1 %copy-start.9 = (f32[128,128]{1,0:T(8,128)S(1)}, f32[128,128]{1,0:T(8,128)}, u32[]{:S(2)}) copy-start(f32[128,128]{1,0:T(8,128)} %param.27) | copy-start | bytes 196612
  50.6 3.4 %copy-start.6 = (f32[1,1,1,128,128]{4,3,2,1,0:T(8,128)S(1)}, f32[1,1,1,128,128]{4,3,2,1,0:T(8,128)}, u32[]{:S(2)}) copy-start(f32[1,1,1,128,128]{4,3,2,1,0:T(8,128)} %param.18) | copy-start | bytes 196612
  54.4 2.1 %copy-start.21 = (s32[1,1,256]{2,1,0:T(1,128)S(1)}, s32[1,1,256]{2,1,0:T(1,128)}, u32[]{:S(2)}) copy-start(s32[1,1,256]{2,1,0:T(1,128)} %copy-done.20) | copy-start | bytes 3076
  54.4 2.4 %copy-start.23 = (s32[1,1,256]{2,1,0:T(1,128)S(1)}, s32[1,1,256]{2,1,0:T(1,128)}, u32[]{:S(2)}) copy-start(s32[1,1,256]{2,1,0:T(1,128)} %copy-done.22) | copy-start | bytes 3076
  54.5 2.8 %copy-start.33 = (f32[128]{0:T(128)S(1)}, f32[128]{0:T(128)}, u32[]{:S(2)}) copy-start(f32[128]{0:T(128)} %copy-done.32) | copy-start | bytes 1540
  54.5 3.2 %copy-start.29 = (f32[128]{0:T(128)S(1)}, f32[128]{0:T(128)}, u32[]{:S(2)}) copy-start(f32[128]{0:T(128)} %copy-done.28) | copy-start | bytes 1540
  55.2 2.8 %copy-start.25 = (f32[1792,1]{0,1:T(1,128)S(1)}, f32[1792,1]{0,1:T(1,128)}, u32[]{:S(2)}) copy-start(f32[1792,1]{0,1:T(1,128)} %reshape.155) | copy-start | bytes 21508
  56.2 4.4 %copy-start.3 = (f32[515,128]{1,0:T(8,128)}, f32[515,128]{1,0:T(8,128)S(1)}, u32[]{:S(2)}) copy-start(f32[515,128]{1,0:T(8,128)S(1)} %fusion.37) | copy-start | bytes 791044
  56.9 3.5 %copy-start.4 = (f32[515,128]{1,0:T(8,128)}, f32[515,128]{1,0:T(8,128)S(1)}, u32[]{:S(2)}) copy-start(f32[515,128]{1,0:T(8,128)S(1)} %fusion.39) | copy-start | bytes 791044
  57.2 2.1 %copy-start.5 = (f32[515,128]{1,0:T(8,128)}, f32[515,128]{1,0:T(8,128)S(1)}, u32[]{:S(2)}) copy-start(f32[515,128]{1,0:T(8,128)S(1)} %fusion.41) | copy-start | bytes 791044
  57.3 2.0 %copy-start.10 = (f32[1,128,128]{2,1,0:T(8,128)S(1)}, f32[1,128,128]{2,1,0:T(8,128)}, u32[]{:S(2)}) copy-start(f32[1,128,128]{2,1,0:T(8,128)} %convolution_bitcast_fusion.13) | copy-start | bytes 196612
  58.0 2.8 %copy-start.27 = (f32[8]{0:T(128)S(1)}, f32[8]{0:T(128)}, u32[]{:S(2)}) copy-start(f32[8]{0:T(128)} %copy-done.26) | copy-start | bytes 100
  58.1 3.3 %copy-start.40 = (f32[128,1792]{1,0:T(8,128)S(1)}, f32[128,1792]{1,0:T(8,128)}, u32[]{:S(2)}) copy-start(f32[128,1792]{1,0:T(8,128)} %copy-done.39) | copy-start | bytes 2752516
  63.4 3.5 %slice-start.2 = ((f32[515,128]{1,0:T(8,128)}), f32[387,128]{1,0:T(8,128)S(1)}, s32[]{:S(2)}) async-start(f32[515,128]{1,0:T(8,128)} %copy-done.5), calls=%async_computation.2 | async-start | bytes 401408 | tf_op jit(solution)/shard_map/transpose(jvp())/split | solution.py:179
  63.4 11.7 %slice-start = ((f32[515,128]{1,0:T(8,128)}), f32[387,128]{1,0:T(8,128)S(1)}, s32[]{:S(2)}) async-start(f32[515,128]{1,0:T(8,128)} %copy-done.3), calls=%async_computation | async-start | bytes 401408 | tf_op jit(solution)/shard_map/transpose(jvp())/split | solution.py:179
  63.4 1.5 %collective-permute-start.6 = (f32[400,128]{1,0:T(8,128)S(1)}, f32[400,128]{1,0:T(8,128)S(1)}, u32[]{:S(2)}, u32[]{:S(2)}) collective-permute-start(f32[400,128]{1,0:T(8,128)S(1)} %slice_select_fusion), channel_id=1, source_target_pairs={{0,32},{32,0},{64,96},{96,64},{128,160},{160,128},{192,224},{224,1... | collective-permute-start | bytes 614408 | tf_op jit(solution)/shard_map/ppermute | solution.py:75
  63.6 23.4 %copy-start.16 = (s32[1792]{0:T(1024)S(1)}, s32[1792]{0:T(1024)}, u32[]{:S(2)}) copy-start(s32[1792]{0:T(1024)} %copy-done.15) | copy-start | bytes 21508
  63.6 29.2 %collective-permute-start.4 = (f32[516,128]{1,0:T(8,128)S(1)}, f32[516,128]{1,0:T(8,128)S(1)}, u32[]{:S(2)}, u32[]{:S(2)}) collective-permute-start(f32[516,128]{1,0:T(8,128)S(1)} %pad_maximum_fusion.12), channel_id=1, source_target_pairs={{24,0},{0,8},{8,16},{16,24},{25,1},{1,9},{9,17},{17,25},{26,2},{2,... | collective-permute-start | bytes 792584 | tf_op jit(solution)/shard_map/ppermute | solution.py:15
  65.0 4.7 %collective-permute-start.7 = (f32[200,128]{1,0:T(8,128)S(1)}, f32[200,128]{1,0:T(8,128)S(1)}, u32[]{:S(2)}, u32[]{:S(2)}) collective-permute-start(f32[200,128]{1,0:T(8,128)S(1)} %slice_select_fusion.1), channel_id=1, source_target_pairs={{0,64},{32,96},{64,0},{96,32},{128,192},{160,224},{192,128},{224,1... | collective-permute-start | bytes 307208 | tf_op jit(solution)/shard_map/ppermute | solution.py:75
  69.7 4.9 %collective-permute-start.8 = (f32[100,128]{1,0:T(8,128)S(1)}, f32[100,128]{1,0:T(8,128)S(1)}, u32[]{:S(2)}, u32[]{:S(2)}) collective-permute-start(f32[100,128]{1,0:T(8,128)S(1)} %slice_select_fusion.2), channel_id=1, source_target_pairs={{0,128},{32,160},{64,192},{96,224},{128,0},{160,32},{192,64},{224,... | collective-permute-start | bytes 153608 | tf_op jit(solution)/shard_map/ppermute | solution.py:75
  71.6 31.1 %copy-start.38 = (f32[8]{0:T(128)S(1)}, f32[8]{0:T(128)}, u32[]{:S(2)}) copy-start(f32[8]{0:T(128)} %param.35) | copy-start | bytes 100
  71.6 21.2 %collective-permute-start.3 = (f32[516,128]{1,0:T(8,128)S(1)}, f32[516,128]{1,0:T(8,128)S(1)}, u32[]{:S(2)}, u32[]{:S(2)}) collective-permute-start(f32[516,128]{1,0:T(8,128)S(1)} %pad_maximum_fusion.11), channel_id=1, source_target_pairs={{224,0},{0,32},{32,64},{64,96},{96,128},{128,160},{160,192},{192,2... | collective-permute-start | bytes 792584 | tf_op jit(solution)/shard_map/ppermute | solution.py:15
  74.6 4.6 %collective-permute-start.9 = (f32[100,128]{1,0:T(8,128)S(1)}, f32[100,128]{1,0:T(8,128)S(1)}, u32[]{:S(2)}, u32[]{:S(2)}) collective-permute-start(f32[100,128]{1,0:T(8,128)S(1)} %select_add_fusion.2), channel_id=1, source_target_pairs={{0,1},{1,0},{2,3},{3,2},{4,5},{5,4},{6,7},{7,6},{8,9},{9,8},{10,11... | collective-permute-start | bytes 153608 | tf_op jit(solution)/shard_map/ppermute | solution.py:77
  79.3 3.0 %collective-permute-start.10 = (f32[100,128]{1,0:T(8,128)S(1)}, f32[100,128]{1,0:T(8,128)S(1)}, u32[]{:S(2)}, u32[]{:S(2)}) collective-permute-start(f32[100,128]{1,0:T(8,128)S(1)} %add.203), channel_id=1, source_target_pairs={{0,2},{1,3},{2,0},{3,1},{4,6},{5,7},{6,4},{7,5},{8,10},{9,11},{10,... | collective-permute-start | bytes 153608 | tf_op jit(solution)/shard_map/ppermute | solution.py:77
  79.9 12.9 %collective-permute-start.5 = (f32[516,128]{1,0:T(8,128)S(1)}, f32[516,128]{1,0:T(8,128)S(1)}, u32[]{:S(2)}, u32[]{:S(2)}) collective-permute-start(f32[516,128]{1,0:T(8,128)S(1)} %pad_maximum_fusion.13), channel_id=1, source_target_pairs={{7,0},{0,1},{1,2},{2,3},{3,4},{4,5},{5,6},{6,7},{15,8},{8,9},{9,10... | collective-permute-start | bytes 792584 | tf_op jit(solution)/shard_map/ppermute | solution.py:15
  82.3 4.6 %collective-permute-start.11 = (f32[100,128]{1,0:T(8,128)S(1)}, f32[100,128]{1,0:T(8,128)S(1)}, u32[]{:S(2)}, u32[]{:S(2)}) collective-permute-start(f32[100,128]{1,0:T(8,128)S(1)} %add.204), channel_id=1, source_target_pairs={{0,4},{1,5},{2,6},{3,7},{4,0},{5,1},{6,2},{7,3},{8,12},{9,13},{10,... | collective-permute-start | bytes 153608 | tf_op jit(solution)/shard_map/ppermute | solution.py:77
  86.9 4.0 %collective-permute-start.12 = (f32[100,128]{1,0:T(8,128)S(1)}, f32[100,128]{1,0:T(8,128)S(1)}, u32[]{:S(2)}, u32[]{:S(2)}) collective-permute-start(f32[100,128]{1,0:T(8,128)S(1)} %add.205), channel_id=1, source_target_pairs={{0,8},{8,0},{16,24},{24,16},{1,9},{9,1},{17,25},{25,17},{2,10},{10... | collective-permute-start | bytes 153608 | tf_op jit(solution)/shard_map/ppermute | solution.py:77
  90.9 7.0 %collective-permute-start.13 = (f32[100,128]{1,0:T(8,128)S(1)}, f32[100,128]{1,0:T(8,128)S(1)}, u32[]{:S(2)}, u32[]{:S(2)}) collective-permute-start(f32[100,128]{1,0:T(8,128)S(1)} %add.206), channel_id=1, source_target_pairs={{0,16},{8,24},{16,0},{24,8},{1,17},{9,25},{17,1},{25,9},{2,18},{10... | collective-permute-start | bytes 153608 | tf_op jit(solution)/shard_map/ppermute | solution.py:77
  97.8 4.6 %collective-permute-start.14 = (f32[100,128]{1,0:T(8,128)S(1)}, f32[100,128]{1,0:T(8,128)S(1)}, u32[]{:S(2)}, u32[]{:S(2)}) collective-permute-start(f32[100,128]{1,0:T(8,128)S(1)} %add.207), channel_id=1, source_target_pairs={{0,128},{32,160},{64,192},{96,224},{128,0},{160,32},{192,64},{224,... | collective-permute-start | bytes 153608 | tf_op jit(solution)/shard_map/ppermute | solution.py:80
  102.4 3.6 %collective-permute-start.15 = (f32[200,128]{1,0:T(8,128)S(1)}, f32[200,128]{1,0:T(8,128)S(1)}, u32[]{:S(2)}, u32[]{:S(2)}) collective-permute-start(f32[200,128]{1,0:T(8,128)S(1)} %maximum_select_fusion.1), channel_id=1, source_target_pairs={{0,64},{32,96},{64,0},{96,32},{128,192},{160,224},{192,128},{224,1... | collective-permute-start | bytes 307208 | tf_op jit(solution)/shard_map/ppermute | solution.py:80
  106.1 16.1 %collective-permute-start.16 = (f32[400,128]{1,0:T(8,128)S(1)}, f32[400,128]{1,0:T(8,128)S(1)}, u32[]{:S(2)}, u32[]{:S(2)}) collective-permute-start(f32[400,128]{1,0:T(8,128)S(1)} %maximum_select_fusion), channel_id=1, source_target_pairs={{0,32},{32,0},{64,96},{96,64},{128,160},{160,128},{192,224},{224,1... | collective-permute-start | bytes 614408 | tf_op jit(solution)/shard_map/ppermute | solution.py:80
  (13 other events, 15.6 us)
where the time goes:
time: 124 us; the launch traced here: 123 us
  starting transfers between devices  38.7 us (31%)
  matrix products  36.4 us (29%)
  waiting for transfers between devices  24.5 us (20%)
  other arithmetic  11.1 us (9%)
  local copies, waits for them, and re-layouts  9.89 us (8%)
  between operations  2.55 us (2%)
    ppermute x3, starting transfers between devices, sum_over_devices(): other = lax.ppermute(padded, axis, [(i, i ^ distance) for i in range(size)])  17.8 us
    ppermute x5, waiting for transfers between devices, sum_over_devices(): lax.ppermute(padded, axis, [(i, i ^ distance) for i in range(size)])  15.7 us
    ppermute x6, starting transfers between devices, from_behind(): return lax.ppermute(block, axis, route)  13 us
    dot_general x15, matrix products, projected(): jnp.dot(matrix.T, table[:channels], precision=lax.Precision.HIGH)  6.07 us
    dot_general x2, matrix products, pair_loss(): center_side = jnp.dot(center_in, center_hot, precision=lax.Precision.HIGH)  5.05 us
    ppermute x3, waiting for transfers between devices, sum_over_devices(): lax.ppermute(send, axis, [(i, i ^ distance) for i in range(size)])  4.75 us
    ppermute x5, starting transfers between devices, sum_over_devices(): lax.ppermute(padded, axis, [(i, i ^ distance) for i in range(size)])  4.2 us
    ppermute x3, waiting for transfers between devices, sum_over_devices(): other = lax.ppermute(padded, axis, [(i, i ^ distance) for i in range(size)])  3.98 us
  transfers between devices with their start and end apart: 17, of which 10 were waited for; matrix products, arithmetic and copies ran while one was open for 16% of the time, Pallas kernels for 0%

commit v1 on v0

--- a/solution.py
+++ b/solution.py
@@ -189,9 +189,15 @@
             axis=1,
         )
         pair_count = center_side.shape[1]
-        displace = (
-            partner_side[channels + vector_rows :] + offset - center_side[channels + vector_rows :]
-        )
+        partner_coords = jnp.concatenate(
+            [
+                jnp.dot(table[channels + vector_rows :], hot, precision=highest)
+                for table, hot in zip(partner_in, partner_hot)
+            ],
+            axis=1,
+        )
+        center_coords = jnp.dot(center_in[channels + vector_rows :], center_hot, precision=highest)
+        displace = partner_coords + offset - center_coords
         energies = edge_energy(
             params_in,
             center_side[:channels],

time: 124 us -> 124 us (level)
  the two profiles are of different devices: /device:TPU:15 before, /device:TPU:33 now
where the time goes in v1:
time: 124 us; the launch traced here: 123 us
  matrix products  37.6 us (30%)
  waiting for transfers between devices  33.8 us (27%)
  starting transfers between devices  31.9 us (26%)
  local copies, waits for them, and re-layouts  9.62 us (8%)
  other arithmetic  7.6 us (6%)
  between operations  2.33 us (2%)
    ppermute x5, waiting for transfers between devices, sum_over_devices(): lax.ppermute(padded, axis, [(i, i ^ distance) for i in range(size)])  19.8 us
    ppermute x6, starting transfers between devices, from_behind(): return lax.ppermute(block, axis, route)  11.2 us
    ppermute x3, starting transfers between devices, sum_over_devices(): other = lax.ppermute(padded, axis, [(i, i ^ distance) for i in range(size)])  10.3 us
    ppermute x3, waiting for transfers between devices, sum_over_devices(): lax.ppermute(send, axis, [(i, i ^ distance) for i in range(size)])  8.14 us
    ppermute x5, starting transfers between devices, sum_over_devices(): lax.ppermute(padded, axis, [(i, i ^ distance) for i in range(size)])  6.79 us
    dot_general x15, matrix products, projected(): jnp.dot(matrix.T, table[:channels], precision=lax.Precision.HIGH)  6.07 us
    ppermute x3, waiting for transfers between devices, sum_over_devices(): other = lax.ppermute(padded, axis, [(i, i ^ distance) for i in range(size)])  5.85 us
    dot_general x3, matrix products, edge_energy(): jnp.dot(read_weight.T, mixed_latent, precision=lax.Precision.HIGH)  3.65 us
  transfers between devices with their start and end apart: 17, of which 11 were waited for; matrix products, arithmetic and copies ran while one was open for 20% of the time, Pallas kernels for 0%

profile of v1, /device:TPU:33, one launch (start us, length us, event | category | flops | bytes accessed | tf_op | source)
XLA Modules:
  0.0 122.8 jit_solution(15833652646142293844)
XLA Ops:
  2.0 2.5 %concatenate.80 = f32[517,128]{1,0:T(8,128)S(1)} concatenate(f32[128,128]{1,0:T(8,128)} %bitcast.328, f32[384,128]{1,0:T(8,128)} %bitcast.325, f32[3,128]{1,0:T(4,128)S(1)} %bitcast.338, f32[1,128]{1,0:T(1,128)} %bitcast.382, f32[1,128]{1,0:T(1,128)S(1)} %convert_bitcast_fusion), dimensions={0} | concatenate | bytes 529408 | tf_op jit(solution)/shard_map/concatenate | solution.py:135
  4.5 5.8 %collective-permute-start.1 = (f32[517,128]{1,0:T(8,128)S(1)}, f32[517,128]{1,0:T(8,128)S(1)}, u32[]{:S(2)}, u32[]{:S(2)}) collective-permute-start(f32[517,128]{1,0:T(8,128)S(1)} %concatenate.80), channel_id=1, source_target_pairs={{8,0},{16,8},{24,16},{0,24},{9,1},{17,9},{25,17},{1,25},{10,2},{18... | collective-permute-start | bytes 794120 | tf_op jit(solution)/shard_map/ppermute | solution.py:15
  10.3 1.2 %collective-permute-start = (f32[517,128]{1,0:T(8,128)S(1)}, f32[517,128]{1,0:T(8,128)S(1)}, u32[]{:S(2)}, u32[]{:S(2)}) collective-permute-start(f32[517,128]{1,0:T(8,128)S(1)} %concatenate.80), channel_id=1, source_target_pairs={{32,0},{64,32},{96,64},{128,96},{160,128},{192,160},{224,192},{0,2... | collective-permute-start | bytes 794120 | tf_op jit(solution)/shard_map/ppermute | solution.py:15
  11.6 0.8 fusion.236
  12.4 0.9 fusion.43
  13.3 0.9 convolution_bitcast_fusion.22
  14.9 1.4 %fusion.238 = (s32[1,1,1,1]{3,2,1,0:T(1,128)}, s32[1,1,1,1]{3,2,1,0:T(1,128)}, s32[1,1,1,1]{3,2,1,0:T(1,128)}, s32[1,1,1,1]{3,2,1,0:T(1,128)}) fusion(s32[1,1,1,4]{3,2,1,0:T(1,128)} %param.26), kind=kLoop, calls=%fused_computation.384 | loop fusion | bytes 32 | tf_op jit(solution)/shard_map/slice | solution.py:153
  17.6 0.8 fusion.237
  18.4 1.0 convolution_reduce_fusion
  19.4 1.1 fusion.216
  20.5 1.1 fusion.214
  21.6 0.8 convolution_bitcast_fusion.30
  22.4 1.0 fusion.17
  23.4 1.0 fusion.16
  24.4 2.1 %fusion.35 = f32[515,1792]{1,0:T(8,128)S(1)} fusion(s32[1792]{0:T(1024)S(1)} %pad_add_fusion.12, f32[3,128]{1,0:T(4,128)S(1)} %bitcast.339, f32[384,128]{1,0:T(8,128)} %bitcast.326, f32[128,128]{1,0:T(8,128)S(1)} %fusion.17), kind=kOutput, calls=%fused_computation.113 | convolution fusion | flops 709133056 | bytes 3962368 | tf_op jit(solution)/shard_map/jvp()/dot_general | solution.py:186
  26.7 1.3 %iota_compare_fusion.52 = (pred[256]{0:T(512)(128)(4,1)S(1)}, pred[256]{0:T(512)(128)(4,1)S(1)}) fusion(s32[]{:T(128)} %bitcast.12, s32[]{:T(128)} %bitcast.11), kind=kLoop, calls=%fused_computation.331 | loop fusion | flops 512 | bytes 520 | tf_op jit(solution)/shard_map/lt | solution.py:153
  34.5 1.0 multiply_add_fusion.2
  36.1 0.8 multiply_reduce_fusion.4
  36.9 0.8 multiply_add_fusion.1
  38.3 0.8 convolution_reduce_fusion.1
  39.1 2.2 %multiply_reduce_fusion.5 = (f32[1792]{0:T(1024)S(1)}, f32[128,1792]{1,0:T(8,128)S(1)}, f32[128,1792]{1,0:T(8,128)}, f32[128,1792]{1,0:T(8,128)S(1)}, f32[128,1792]{1,0:T(8,128)S(1)}) fusion(f32[128,1792]{1,0:T(8,128)S(1)} %get-tuple-element.11, f32[128,1792]{1,0:T(8,128)S(1)} %get-tuple-element.62, f32[128,1792]{1,0:T(8,128)S(1)} %get-tuple-element.12, ...), kind=kOutput, calls=%fused_computation.101 | convolution fusion | flops 180746496 | bytes 9262592 | tf_op jit(solution)/shard_map/transpose(jvp())/dot_general | solution.py:41
  43.9 1.1 fusion.31
  45.4 0.8 multiply_reduce_fusion
  47.6 1.2 fusion.3
  48.8 1.2 fusion.15
  54.1 0.9 convolution_bitcast_fusion.28
  55.3 1.9 %collective-permute-start.5 = (f32[516,128]{1,0:T(8,128)S(1)}, f32[516,128]{1,0:T(8,128)S(1)}, u32[]{:S(2)}, u32[]{:S(2)}) collective-permute-start(f32[516,128]{1,0:T(8,128)S(1)} %pad_maximum_fusion.13), channel_id=1, source_target_pairs={{7,0},{0,1},{1,2},{2,3},{3,4},{4,5},{5,6},{6,7},{15,8},{8,9},{9,10... | collective-permute-start | bytes 792584 | tf_op jit(solution)/shard_map/ppermute | solution.py:15
  57.3 1.0 fusion.119
  59.4 1.0 constant_dynamic-update-slice_fusion.2
  60.6 0.9 convolution_dynamic-update-slice_fusion
  61.5 2.3 %collective-permute-start.6 = (f32[400,128]{1,0:T(8,128)S(1)}, f32[400,128]{1,0:T(8,128)S(1)}, u32[]{:S(2)}, u32[]{:S(2)}) collective-permute-start(f32[400,128]{1,0:T(8,128)S(1)} %slice_select_fusion), channel_id=1, source_target_pairs={{0,32},{32,0},{64,96},{96,64},{128,160},{160,128},{192,224},{224,1... | collective-permute-start | bytes 614408 | tf_op jit(solution)/shard_map/ppermute | solution.py:75
  63.9 0.9 collective-permute-done.6
  65.1 4.0 %collective-permute-done.7 = f32[200,128]{1,0:T(8,128)S(1)} collective-permute-done((f32[200,128]{1,0:T(8,128)S(1)}, f32[200,128]{1,0:T(8,128)S(1)}, u32[]{:S(2)}, u32[]{:S(2)}) %collective-permute-start.7) | collective-permute-done | bytes 102432 | tf_op jit(solution)/shard_map/ppermute | solution.py:75
  69.1 1.3 %collective-permute-start.8 = (f32[100,128]{1,0:T(8,128)S(1)}, f32[100,128]{1,0:T(8,128)S(1)}, u32[]{:S(2)}, u32[]{:S(2)}) collective-permute-start(f32[100,128]{1,0:T(8,128)S(1)} %slice_select_fusion.2), channel_id=1, source_target_pairs={{0,128},{32,160},{64,192},{96,224},{128,0},{160,32},{192,64},{224,... | collective-permute-start | bytes 153608 | tf_op jit(solution)/shard_map/ppermute | solution.py:75
  70.5 3.2 %collective-permute-done.8 = f32[100,128]{1,0:T(8,128)S(1)} collective-permute-done((f32[100,128]{1,0:T(8,128)S(1)}, f32[100,128]{1,0:T(8,128)S(1)}, u32[]{:S(2)}, u32[]{:S(2)}) %collective-permute-start.8) | collective-permute-done | bytes 51232 | tf_op jit(solution)/shard_map/ppermute | solution.py:75
  73.7 1.1 collective-permute-start.9
  74.9 9.5 %collective-permute-done.9 = f32[100,128]{1,0:T(8,128)S(1)} collective-permute-done((f32[100,128]{1,0:T(8,128)S(1)}, f32[100,128]{1,0:T(8,128)S(1)}, u32[]{:S(2)}, u32[]{:S(2)}) %collective-permute-start.9) | collective-permute-done | bytes 51232 | tf_op jit(solution)/shard_map/ppermute | solution.py:77
  84.5 2.1 %collective-permute-start.3 = (f32[516,128]{1,0:T(8,128)S(1)}, f32[516,128]{1,0:T(8,128)S(1)}, u32[]{:S(2)}, u32[]{:S(2)}) collective-permute-start(f32[516,128]{1,0:T(8,128)S(1)} %pad_maximum_fusion.11), channel_id=1, source_target_pairs={{224,0},{0,32},{32,64},{64,96},{96,128},{128,160},{160,192},{192,2... | collective-permute-start | bytes 792584 | tf_op jit(solution)/shard_map/ppermute | solution.py:15
  86.6 0.8 collective-permute-done.10
  87.8 4.5 %collective-permute-done.11 = f32[100,128]{1,0:T(8,128)S(1)} collective-permute-done((f32[100,128]{1,0:T(8,128)S(1)}, f32[100,128]{1,0:T(8,128)S(1)}, u32[]{:S(2)}, u32[]{:S(2)}) %collective-permute-start.11) | collective-permute-done | bytes 51232 | tf_op jit(solution)/shard_map/ppermute | solution.py:77
  92.2 1.0 collective-permute-start.12
  93.6 2.6 %collective-permute-done.12 = f32[100,128]{1,0:T(8,128)S(1)} collective-permute-done((f32[100,128]{1,0:T(8,128)S(1)}, f32[100,128]{1,0:T(8,128)S(1)}, u32[]{:S(2)}, u32[]{:S(2)}) %collective-permute-start.12) | collective-permute-done | bytes 51232 | tf_op jit(solution)/shard_map/ppermute | solution.py:77
  96.2 4.5 %collective-permute-start.13 = (f32[100,128]{1,0:T(8,128)S(1)}, f32[100,128]{1,0:T(8,128)S(1)}, u32[]{:S(2)}, u32[]{:S(2)}) collective-permute-start(f32[100,128]{1,0:T(8,128)S(1)} %add.212), channel_id=1, source_target_pairs={{0,16},{8,24},{16,0},{24,8},{1,17},{9,25},{17,1},{25,9},{2,18},{10... | collective-permute-start | bytes 153608 | tf_op jit(solution)/shard_map/ppermute | solution.py:77
  100.8 2.4 %collective-permute-done.13 = f32[100,128]{1,0:T(8,128)S(1)} collective-permute-done((f32[100,128]{1,0:T(8,128)S(1)}, f32[100,128]{1,0:T(8,128)S(1)}, u32[]{:S(2)}, u32[]{:S(2)}) %collective-permute-start.13) | collective-permute-done | bytes 51232 | tf_op jit(solution)/shard_map/ppermute | solution.py:77
  104.9 3.0 %collective-permute-done.14 = f32[100,128]{1,0:T(8,128)S(1)} collective-permute-done((f32[100,128]{1,0:T(8,128)S(1)}, f32[100,128]{1,0:T(8,128)S(1)}, u32[]{:S(2)}, u32[]{:S(2)}) %collective-permute-start.14) | collective-permute-done | bytes 51232 | tf_op jit(solution)/shard_map/ppermute | solution.py:80
  109.0 2.4 %collective-permute-done.15 = f32[200,128]{1,0:T(8,128)S(1)} collective-permute-done((f32[200,128]{1,0:T(8,128)S(1)}, f32[200,128]{1,0:T(8,128)S(1)}, u32[]{:S(2)}, u32[]{:S(2)}) %collective-permute-start.15) | collective-permute-done | bytes 102432 | tf_op jit(solution)/shard_map/ppermute | solution.py:80
  111.5 9.4 %collective-permute-start.16 = (f32[400,128]{1,0:T(8,128)S(1)}, f32[400,128]{1,0:T(8,128)S(1)}, u32[]{:S(2)}, u32[]{:S(2)}) collective-permute-start(f32[400,128]{1,0:T(8,128)S(1)} %maximum_select_fusion), channel_id=1, source_target_pairs={{0,32},{32,0},{64,96},{96,64},{128,160},{160,128},{192,224},{224,1... | collective-permute-start | bytes 614408 | tf_op jit(solution)/shard_map/ppermute | solution.py:80
  122.0 0.8 fusion.53
  (187 shorter events, 25.4 us)
Async XLA Ops:
  0.6 37.1 %copy-start = (f32[128,128]{1,0:T(8,128)S(1)}, f32[128,128]{1,0:T(8,128)}, u32[]{:S(2)}) copy-start(f32[128,128]{1,0:T(8,128)} %param.33) | copy-start | bytes 196612
  4.5 24.3 %collective-permute-start.2 = (f32[517,128]{1,0:T(8,128)S(1)}, f32[517,128]{1,0:T(8,128)S(1)}, u32[]{:S(2)}, u32[]{:S(2)}) collective-permute-start(f32[517,128]{1,0:T(8,128)S(1)} %concatenate.80), channel_id=1, source_target_pairs={{1,0},{2,1},{3,2},{4,3},{5,4},{6,5},{7,6},{0,7},{9,8},{10,9},{11,1... | collective-permute-start | bytes 794120 | tf_op jit(solution)/shard_map/ppermute | solution.py:15
  4.5 24.8 %collective-permute-start.1 = (f32[517,128]{1,0:T(8,128)S(1)}, f32[517,128]{1,0:T(8,128)S(1)}, u32[]{:S(2)}, u32[]{:S(2)}) collective-permute-start(f32[517,128]{1,0:T(8,128)S(1)} %concatenate.80), channel_id=1, source_target_pairs={{8,0},{16,8},{24,16},{0,24},{9,1},{17,9},{25,17},{1,25},{10,2},{18... | collective-permute-start | bytes 794120 | tf_op jit(solution)/shard_map/ppermute | solution.py:15
  10.3 19.4 %collective-permute-start = (f32[517,128]{1,0:T(8,128)S(1)}, f32[517,128]{1,0:T(8,128)S(1)}, u32[]{:S(2)}, u32[]{:S(2)}) collective-permute-start(f32[517,128]{1,0:T(8,128)S(1)} %concatenate.80), channel_id=1, source_target_pairs={{32,0},{64,32},{96,64},{128,96},{160,128},{192,160},{224,192},{0,2... | collective-permute-start | bytes 794120 | tf_op jit(solution)/shard_map/ppermute | solution.py:15
  26.4 1.6 %copy-start.7 = (f32[1,1,1,3,128,128]{5,4,3,2,1,0:T(8,128)S(1)}, f32[1,1,1,3,128,128]{5,4,3,2,1,0:T(8,128)}, u32[]{:S(2)}) copy-start(f32[1,1,1,3,128,128]{5,4,3,2,1,0:T(8,128)} %param.19) | copy-start | bytes 589828
  26.5 2.5 %copy-start.18 = (f32[2,8,128]{2,1,0:T(8,128)S(1)}, f32[2,8,128]{2,1,0:T(8,128)}, u32[]{:S(2)}) copy-start(f32[2,8,128]{2,1,0:T(8,128)} %param.30) | copy-start | bytes 24580
  26.5 3.6 %copy-start.21 = (f32[1,1,1,3,128]{4,2,3,1,0:T(1,128)S(1)}, f32[1,1,1,3,128]{4,2,3,1,0:T(1,128)}, u32[]{:S(2)}) copy-start(f32[1,1,1,3,128]{4,2,3,1,0:T(1,128)} %param.20) | copy-start | bytes 4612
  26.7 4.6 %copy-start.1 = (f32[128,128]{1,0:T(8,128)S(1)}, f32[128,128]{1,0:T(8,128)}, u32[]{:S(2)}) copy-start(f32[128,128]{1,0:T(8,128)} %param.28) | copy-start | bytes 196612
  29.7 3.5 %copy-start.16 = (f32[517,128]{1,0:T(8,128)}, f32[517,128]{1,0:T(8,128)S(1)}, u32[]{:S(2)}) copy-start(f32[517,128]{1,0:T(8,128)S(1)} %collective-permute-done) | copy-start | bytes 794116
  33.0 0.7 copy-start.19
  33.7 0.8 copy-start.23
  34.5 9.3 %copy-start.11 = (f32[128,1792]{1,0:T(8,128)}, f32[128,1792]{1,0:T(8,128)S(1)}, u32[]{:S(2)}) copy-start(f32[128,1792]{1,0:T(8,128)S(1)} %fusion.7) | copy-start | bytes 2752516
  34.5 1.0 copy-start.15
  35.5 8.4 %copy-start.25 = (f32[128,1792]{1,0:T(8,128)}, f32[128,1792]{1,0:T(8,128)S(1)}, u32[]{:S(2)}) copy-start(f32[128,1792]{1,0:T(8,128)S(1)} %get-tuple-element.61) | copy-start | bytes 2752516
  36.9 1.4 %copy-start.22 = (f32[128]{0:T(128)S(1)}, f32[128]{0:T(128)}, u32[]{:S(2)}) copy-start(f32[128]{0:T(128)} %param.34) | copy-start | bytes 1540
  37.7 1.4 %copy-start.2 = (f32[128,1792]{1,0:T(8,128)}, f32[128,1792]{1,0:T(8,128)S(1)}, u32[]{:S(2)}) copy-start(f32[128,1792]{1,0:T(8,128)S(1)} %get-tuple-element.13) | copy-start | bytes 2752516
  38.3 3.0 %copy-start.4 = (f32[128,1792]{1,0:T(8,128)}, f32[128,1792]{1,0:T(8,128)S(1)}, u32[]{:S(2)}) copy-start(f32[128,1792]{1,0:T(8,128)S(1)} %convolution_bitcast_fusion.4) | copy-start | bytes 2752516
  43.8 1.2 copy-start.13
  45.4 2.2 %copy-start.6 = (f32[128,1792]{1,0:T(8,128)S(1)}, f32[128,1792]{1,0:T(8,128)}, u32[]{:S(2)}) copy-start(f32[128,1792]{1,0:T(8,128)} %get-tuple-element.17) | copy-start | bytes 2752516
  48.8 1.2 copy-start.20
  48.8 1.3 %copy-start.17 = (f32[128,128]{1,0:T(8,128)S(1)}, f32[128,128]{1,0:T(8,128)}, u32[]{:S(2)}) copy-start(f32[128,128]{1,0:T(8,128)} %param.27) | copy-start | bytes 196612
  50.0 1.3 %copy-start.10 = (f32[1,1,1,128,128]{4,3,2,1,0:T(8,128)S(1)}, f32[1,1,1,128,128]{4,3,2,1,0:T(8,128)}, u32[]{:S(2)}) copy-start(f32[1,1,1,128,128]{4,3,2,1,0:T(8,128)} %param.18) | copy-start | bytes 196612
  52.0 5.3 %copy-start.8 = (f32[515,128]{1,0:T(8,128)}, f32[515,128]{1,0:T(8,128)S(1)}, u32[]{:S(2)}) copy-start(f32[515,128]{1,0:T(8,128)S(1)} %convolution_add_fusion.2) | copy-start | bytes 791044
  52.7 1.3 %copy-start.5 = (f32[128,1792]{1,0:T(8,128)S(1)}, f32[128,1792]{1,0:T(8,128)}, u32[]{:S(2)}) copy-start(f32[128,1792]{1,0:T(8,128)} %copy-done.4) | copy-start | bytes 2752516
  53.4 4.9 %copy-start.9 = (f32[515,128]{1,0:T(8,128)}, f32[515,128]{1,0:T(8,128)S(1)}, u32[]{:S(2)}) copy-start(f32[515,128]{1,0:T(8,128)S(1)} %convolution_add_fusion.1) | copy-start | bytes 791044
  54.1 5.3 %copy-start.12 = (f32[128,1792]{1,0:T(8,128)S(1)}, f32[128,1792]{1,0:T(8,128)}, u32[]{:S(2)}) copy-start(f32[128,1792]{1,0:T(8,128)} %copy-done.11) | copy-start | bytes 2752516
  54.1 5.3 %copy-start.14 = (f32[128,1792]{1,0:T(8,128)S(1)}, f32[128,1792]{1,0:T(8,128)}, u32[]{:S(2)}) copy-start(f32[128,1792]{1,0:T(8,128)} %copy-done.13) | copy-start | bytes 2752516
  54.1 5.3 %copy-start.26 = (f32[128,1792]{1,0:T(8,128)S(1)}, f32[128,1792]{1,0:T(8,128)}, u32[]{:S(2)}) copy-start(f32[128,1792]{1,0:T(8,128)} %copy-done.25) | copy-start | bytes 2752516
  55.3 45.4 %collective-permute-start.5 = (f32[516,128]{1,0:T(8,128)S(1)}, f32[516,128]{1,0:T(8,128)S(1)}, u32[]{:S(2)}, u32[]{:S(2)}) collective-permute-start(f32[516,128]{1,0:T(8,128)S(1)} %pad_maximum_fusion.13), channel_id=1, source_target_pairs={{7,0},{0,1},{1,2},{2,3},{3,4},{4,5},{5,6},{6,7},{15,8},{8,9},{9,10... | collective-permute-start | bytes 792584 | tf_op jit(solution)/shard_map/ppermute | solution.py:15
  59.4 1.2 copy-start.3
  60.6 4.5 %slice-start.1 = ((f32[515,128]{1,0:T(8,128)}), f32[387,128]{1,0:T(8,128)S(1)}, s32[]{:S(2)}) async-start(f32[515,128]{1,0:T(8,128)} %copy-done.9), calls=%async_computation.1 | async-start | bytes 401408 | tf_op jit(solution)/shard_map/transpose(jvp())/split | solution.py:179
  61.4 13.4 %slice-start = ((f32[515,128]{1,0:T(8,128)}), f32[387,128]{1,0:T(8,128)S(1)}, s32[]{:S(2)}) async-start(f32[515,128]{1,0:T(8,128)} %copy-done.8), calls=%async_computation | async-start | bytes 401408 | tf_op jit(solution)/shard_map/transpose(jvp())/split | solution.py:179
  61.5 3.3 %collective-permute-start.6 = (f32[400,128]{1,0:T(8,128)S(1)}, f32[400,128]{1,0:T(8,128)S(1)}, u32[]{:S(2)}, u32[]{:S(2)}) collective-permute-start(f32[400,128]{1,0:T(8,128)S(1)} %slice_select_fusion), channel_id=1, source_target_pairs={{0,32},{32,0},{64,96},{96,64},{128,160},{160,128},{192,224},{224,1... | collective-permute-start | bytes 614408 | tf_op jit(solution)/shard_map/ppermute | solution.py:75
  64.9 4.2 %collective-permute-start.7 = (f32[200,128]{1,0:T(8,128)S(1)}, f32[200,128]{1,0:T(8,128)S(1)}, u32[]{:S(2)}, u32[]{:S(2)}) collective-permute-start(f32[200,128]{1,0:T(8,128)S(1)} %slice_select_fusion.1), channel_id=1, source_target_pairs={{0,64},{32,96},{64,0},{96,32},{128,192},{160,224},{192,128},{224,1... | collective-permute-start | bytes 307208 | tf_op jit(solution)/shard_map/ppermute | solution.py:75
  69.1 4.6 %collective-permute-start.8 = (f32[100,128]{1,0:T(8,128)S(1)}, f32[100,128]{1,0:T(8,128)S(1)}, u32[]{:S(2)}, u32[]{:S(2)}) collective-permute-start(f32[100,128]{1,0:T(8,128)S(1)} %slice_select_fusion.2), channel_id=1, source_target_pairs={{0,128},{32,160},{64,192},{96,224},{128,0},{160,32},{192,64},{224,... | collective-permute-start | bytes 153608 | tf_op jit(solution)/shard_map/ppermute | solution.py:75
  70.4 38.0 %copy-start.24 = (f32[8]{0:T(128)S(1)}, f32[8]{0:T(128)}, u32[]{:S(2)}) copy-start(f32[8]{0:T(128)} %param.35) | copy-start | bytes 100
  70.4 30.3 %collective-permute-start.4 = (f32[516,128]{1,0:T(8,128)S(1)}, f32[516,128]{1,0:T(8,128)S(1)}, u32[]{:S(2)}, u32[]{:S(2)}) collective-permute-start(f32[516,128]{1,0:T(8,128)S(1)} %pad_maximum_fusion.12), channel_id=1, source_target_pairs={{24,0},{0,8},{8,16},{16,24},{25,1},{1,9},{9,17},{17,25},{26,2},{2,... | collective-permute-start | bytes 792584 | tf_op jit(solution)/shard_map/ppermute | solution.py:15
  73.7 10.6 %collective-permute-start.9 = (f32[100,128]{1,0:T(8,128)S(1)}, f32[100,128]{1,0:T(8,128)S(1)}, u32[]{:S(2)}, u32[]{:S(2)}) collective-permute-start(f32[100,128]{1,0:T(8,128)S(1)} %select_add_fusion.2), channel_id=1, source_target_pairs={{0,1},{1,0},{2,3},{3,2},{4,5},{5,4},{6,7},{7,6},{8,9},{9,8},{10,11... | collective-permute-start | bytes 153608 | tf_op jit(solution)/shard_map/ppermute | solution.py:77
  84.3 3.1 %collective-permute-start.10 = (f32[100,128]{1,0:T(8,128)S(1)}, f32[100,128]{1,0:T(8,128)S(1)}, u32[]{:S(2)}, u32[]{:S(2)}) collective-permute-start(f32[100,128]{1,0:T(8,128)S(1)} %add.209), channel_id=1, source_target_pairs={{0,2},{1,3},{2,0},{3,1},{4,6},{5,7},{6,4},{7,5},{8,10},{9,11},{10,... | collective-permute-start | bytes 153608 | tf_op jit(solution)/shard_map/ppermute | solution.py:77
  84.5 16.2 %collective-permute-start.3 = (f32[516,128]{1,0:T(8,128)S(1)}, f32[516,128]{1,0:T(8,128)S(1)}, u32[]{:S(2)}, u32[]{:S(2)}) collective-permute-start(f32[516,128]{1,0:T(8,128)S(1)} %pad_maximum_fusion.11), channel_id=1, source_target_pairs={{224,0},{0,32},{32,64},{64,96},{96,128},{128,160},{160,192},{192,2... | collective-permute-start | bytes 792584 | tf_op jit(solution)/shard_map/ppermute | solution.py:15
  87.4 4.8 %collective-permute-start.11 = (f32[100,128]{1,0:T(8,128)S(1)}, f32[100,128]{1,0:T(8,128)S(1)}, u32[]{:S(2)}, u32[]{:S(2)}) collective-permute-start(f32[100,128]{1,0:T(8,128)S(1)} %add.210), channel_id=1, source_target_pairs={{0,4},{1,5},{2,6},{3,7},{4,0},{5,1},{6,2},{7,3},{8,12},{9,13},{10,... | collective-permute-start | bytes 153608 | tf_op jit(solution)/shard_map/ppermute | solution.py:77
  92.2 4.0 %collective-permute-start.12 = (f32[100,128]{1,0:T(8,128)S(1)}, f32[100,128]{1,0:T(8,128)S(1)}, u32[]{:S(2)}, u32[]{:S(2)}) collective-permute-start(f32[100,128]{1,0:T(8,128)S(1)} %add.211), channel_id=1, source_target_pairs={{0,8},{8,0},{16,24},{24,16},{1,9},{9,1},{17,25},{25,17},{2,10},{10... | collective-permute-start | bytes 153608 | tf_op jit(solution)/shard_map/ppermute | solution.py:77
  96.2 7.0 %collective-permute-start.13 = (f32[100,128]{1,0:T(8,128)S(1)}, f32[100,128]{1,0:T(8,128)S(1)}, u32[]{:S(2)}, u32[]{:S(2)}) collective-permute-start(f32[100,128]{1,0:T(8,128)S(1)} %add.212), channel_id=1, source_target_pairs={{0,16},{8,24},{16,0},{24,8},{1,17},{9,25},{17,1},{25,9},{2,18},{10... | collective-permute-start | bytes 153608 | tf_op jit(solution)/shard_map/ppermute | solution.py:77
  103.3 4.6 %collective-permute-start.14 = (f32[100,128]{1,0:T(8,128)S(1)}, f32[100,128]{1,0:T(8,128)S(1)}, u32[]{:S(2)}, u32[]{:S(2)}) collective-permute-start(f32[100,128]{1,0:T(8,128)S(1)} %add.213), channel_id=1, source_target_pairs={{0,128},{32,160},{64,192},{96,224},{128,0},{160,32},{192,64},{224,... | collective-permute-start | bytes 153608 | tf_op jit(solution)/shard_map/ppermute | solution.py:80
  107.9 3.6 %collective-permute-start.15 = (f32[200,128]{1,0:T(8,128)S(1)}, f32[200,128]{1,0:T(8,128)S(1)}, u32[]{:S(2)}, u32[]{:S(2)}) collective-permute-start(f32[200,128]{1,0:T(8,128)S(1)} %maximum_select_fusion.1), channel_id=1, source_target_pairs={{0,64},{32,96},{64,0},{96,32},{128,192},{160,224},{192,128},{224,1... | collective-permute-start | bytes 307208 | tf_op jit(solution)/shard_map/ppermute | solution.py:80
  111.5 10.5 %collective-permute-start.16 = (f32[400,128]{1,0:T(8,128)S(1)}, f32[400,128]{1,0:T(8,128)S(1)}, u32[]{:S(2)}, u32[]{:S(2)}) collective-permute-start(f32[400,128]{1,0:T(8,128)S(1)} %maximum_select_fusion), channel_id=1, source_target_pairs={{0,32},{32,0},{64,96},{96,64},{128,160},{160,128},{192,224},{224,1... | collective-permute-start | bytes 614408 | tf_op jit(solution)/shard_map/ppermute | solution.py:80

commit v2 on v1

--- a/solution.py
+++ b/solution.py
@@ -60,6 +60,14 @@
     return steps
 
 
+def exchange_partner(index, distance, size):
+    if distance >= 2 and 2 * distance == size:
+        unit = distance // 2
+        digit, low = divmod(index, unit)
+        return (3 - digit) * unit + low
+    return index ^ distance
+
+
 def sum_over_devices(rows):
     steps = halving_steps()
     if any(size & (size - 1) for _, _, size in steps):
@@ -74,7 +82,7 @@
         send = jnp.where(upper, low, high)
         padded = keep + lax.ppermute(send, axis, [(i, i ^ distance) for i in range(size)])
     for axis, distance, size in steps[halvings:]:
-        padded = padded + lax.ppermute(padded, axis, [(i, i ^ distance) for i in range(size)])
+        padded = padded + lax.ppermute(padded, axis, [(i, exchange_partner(i, distance, size)) for i in range(size)])
     for axis, distance, size in reversed(steps[:halvings]):
         upper = (lax.axis_index(axis) // distance) % 2 == 1
         other = lax.ppermute(padded, axis, [(i, i ^ distance) for i in range(size)])

time: 124 us -> 121 us (0.976)
  waiting for transfers between devices: 33.8 us -> 31.7 us
    ppermute x5, waiting for transfers between devices: 19.8 us -> 18.3 us  [sum_over_devices(): lax.ppermute(padded, axis, [(i, exchange_partner(i, distance, size)) for...]
  transfers between devices with their start and end apart: 17 -> 17, of which waited for: 11 -> 11; matrix products, arithmetic and copies ran while one was open for 20% -> 21% of each run, Pallas kernels for 0% -> 0%
where the time goes in v2:
time: 121 us; the launch traced here: 120 us
  matrix products  37.6 us (31%)
  waiting for transfers between devices  31.7 us (26%)
  starting transfers between devices  31.6 us (26%)
  local copies, waits for them, and re-layouts  9.62 us (8%)
  other arithmetic  7.6 us (6%)
  between operations  2.33 us (2%)
    ppermute x5, waiting for transfers between devices, sum_over_devices(): lax.ppermute(padded, axis, [(i, exchange_partner(i, distance, size)) for...  18.3 us
    ppermute x6, starting transfers between devices, from_behind(): return lax.ppermute(block, axis, route)  11.2 us
    ppermute x3, starting transfers between devices, sum_over_devices(): other = lax.ppermute(padded, axis, [(i, i ^ distance) for i in range(size)])  10.5 us
    ppermute x3, waiting for transfers between devices, sum_over_devices(): lax.ppermute(send, axis, [(i, i ^ distance) for i in range(size)])  8.14 us
    ppermute x5, starting transfers between devices, sum_over_devices(): lax.ppermute(padded, axis, [(i, exchange_partner(i, distance, size)) for...  6.23 us
    dot_general x15, matrix products, projected(): jnp.dot(matrix.T, table[:channels], precision=lax.Precision.HIGH)  6.07 us
    ppermute x3, waiting for transfers between devices, sum_over_devices(): other = lax.ppermute(padded, axis, [(i, i ^ distance) for i in range(size)])  5.24 us
    dot_general x3, matrix products, edge_energy(): jnp.dot(read_weight.T, mixed_latent, precision=lax.Precision.HIGH)  3.65 us
  transfers between devices with their start and end apart: 17, of which 11 were waited for; matrix products, arithmetic and copies ran while one was open for 21% of the time, Pallas kernels for 0%

profile of v2, /device:TPU:33, one launch (start us, length us, event | category | flops | bytes accessed | tf_op | source)
XLA Modules:
  0.0 120.4 jit_solution(6390126840429068338)
XLA Ops:
  2.0 2.5 %concatenate.80 = f32[517,128]{1,0:T(8,128)S(1)} concatenate(f32[128,128]{1,0:T(8,128)} %bitcast.328, f32[384,128]{1,0:T(8,128)} %bitcast.325, f32[3,128]{1,0:T(4,128)S(1)} %bitcast.338, f32[1,128]{1,0:T(1,128)} %bitcast.382, f32[1,128]{1,0:T(1,128)S(1)} %convert_bitcast_fusion), dimensions={0} | concatenate | bytes 529408 | tf_op jit(solution)/shard_map/concatenate | solution.py:143
  4.5 5.8 %collective-permute-start.1 = (f32[517,128]{1,0:T(8,128)S(1)}, f32[517,128]{1,0:T(8,128)S(1)}, u32[]{:S(2)}, u32[]{:S(2)}) collective-permute-start(f32[517,128]{1,0:T(8,128)S(1)} %concatenate.80), channel_id=1, source_target_pairs={{8,0},{16,8},{24,16},{0,24},{9,1},{17,9},{25,17},{1,25},{10,2},{18... | collective-permute-start | bytes 794120 | tf_op jit(solution)/shard_map/ppermute | solution.py:15
  10.3 1.2 %collective-permute-start = (f32[517,128]{1,0:T(8,128)S(1)}, f32[517,128]{1,0:T(8,128)S(1)}, u32[]{:S(2)}, u32[]{:S(2)}) collective-permute-start(f32[517,128]{1,0:T(8,128)S(1)} %concatenate.80), channel_id=1, source_target_pairs={{32,0},{64,32},{96,64},{128,96},{160,128},{192,160},{224,192},{0,2... | collective-permute-start | bytes 794120 | tf_op jit(solution)/shard_map/ppermute | solution.py:15
  11.6 0.8 fusion.236
  12.4 0.9 fusion.43
  13.3 0.9 convolution_bitcast_fusion.22
  14.9 1.4 %fusion.238 = (s32[1,1,1,1]{3,2,1,0:T(1,128)}, s32[1,1,1,1]{3,2,1,0:T(1,128)}, s32[1,1,1,1]{3,2,1,0:T(1,128)}, s32[1,1,1,1]{3,2,1,0:T(1,128)}) fusion(s32[1,1,1,4]{3,2,1,0:T(1,128)} %param.26), kind=kLoop, calls=%fused_computation.384 | loop fusion | bytes 32 | tf_op jit(solution)/shard_map/slice | solution.py:161
  17.6 0.8 fusion.237
  18.4 1.0 convolution_reduce_fusion
  19.4 1.1 fusion.216
  20.5 1.1 fusion.214
  21.6 0.8 convolution_bitcast_fusion.30
  22.4 1.0 fusion.17
  23.4 1.0 fusion.16
  24.4 2.1 %fusion.35 = f32[515,1792]{1,0:T(8,128)S(1)} fusion(s32[1792]{0:T(1024)S(1)} %pad_add_fusion.12, f32[3,128]{1,0:T(4,128)S(1)} %bitcast.339, f32[384,128]{1,0:T(8,128)} %bitcast.326, f32[128,128]{1,0:T(8,128)S(1)} %fusion.17), kind=kOutput, calls=%fused_computation.113 | convolution fusion | flops 709133056 | bytes 3962368 | tf_op jit(solution)/shard_map/jvp()/dot_general | solution.py:194
  26.7 1.3 %iota_compare_fusion.52 = (pred[256]{0:T(512)(128)(4,1)S(1)}, pred[256]{0:T(512)(128)(4,1)S(1)}) fusion(s32[]{:T(128)} %bitcast.12, s32[]{:T(128)} %bitcast.11), kind=kLoop, calls=%fused_computation.331 | loop fusion | flops 512 | bytes 520 | tf_op jit(solution)/shard_map/lt | solution.py:161
  34.5 1.0 multiply_add_fusion.2
  36.1 0.8 multiply_reduce_fusion.4
  36.9 0.8 multiply_add_fusion.1
  38.3 0.8 convolution_reduce_fusion.1
  39.1 2.2 %multiply_reduce_fusion.5 = (f32[1792]{0:T(1024)S(1)}, f32[128,1792]{1,0:T(8,128)S(1)}, f32[128,1792]{1,0:T(8,128)}, f32[128,1792]{1,0:T(8,128)S(1)}, f32[128,1792]{1,0:T(8,128)S(1)}) fusion(f32[128,1792]{1,0:T(8,128)S(1)} %get-tuple-element.11, f32[128,1792]{1,0:T(8,128)S(1)} %get-tuple-element.62, f32[128,1792]{1,0:T(8,128)S(1)} %get-tuple-element.12, ...), kind=kOutput, calls=%fused_computation.101 | convolution fusion | flops 180746496 | bytes 9262592 | tf_op jit(solution)/shard_map/transpose(jvp())/dot_general | solution.py:41
  43.9 1.1 fusion.31
  47.6 1.2 fusion.3
  48.8 1.2 fusion.15
  54.1 0.9 convolution_bitcast_fusion.28
  55.3 1.9 %collective-permute-start.5 = (f32[516,128]{1,0:T(8,128)S(1)}, f32[516,128]{1,0:T(8,128)S(1)}, u32[]{:S(2)}, u32[]{:S(2)}) collective-permute-start(f32[516,128]{1,0:T(8,128)S(1)} %pad_maximum_fusion.13), channel_id=1, source_target_pairs={{7,0},{0,1},{1,2},{2,3},{3,4},{4,5},{5,6},{6,7},{15,8},{8,9},{9,10... | collective-permute-start | bytes 792584 | tf_op jit(solution)/shard_map/ppermute | solution.py:15
  57.3 1.0 fusion.119
  59.4 1.0 constant_dynamic-update-slice_fusion.2
  60.6 0.9 convolution_dynamic-update-slice_fusion
  61.5 2.3 %collective-permute-start.6 = (f32[400,128]{1,0:T(8,128)S(1)}, f32[400,128]{1,0:T(8,128)S(1)}, u32[]{:S(2)}, u32[]{:S(2)}) collective-permute-start(f32[400,128]{1,0:T(8,128)S(1)} %slice_select_fusion), channel_id=1, source_target_pairs={{0,32},{32,0},{64,96},{96,64},{128,160},{160,128},{192,224},{224,1... | collective-permute-start | bytes 614408 | tf_op jit(solution)/shard_map/ppermute | solution.py:83
  63.9 0.9 collective-permute-done.6
  65.1 4.0 %collective-permute-done.7 = f32[200,128]{1,0:T(8,128)S(1)} collective-permute-done((f32[200,128]{1,0:T(8,128)S(1)}, f32[200,128]{1,0:T(8,128)S(1)}, u32[]{:S(2)}, u32[]{:S(2)}) %collective-permute-start.7) | collective-permute-done | bytes 102432 | tf_op jit(solution)/shard_map/ppermute | solution.py:83
  69.1 1.3 %collective-permute-start.8 = (f32[100,128]{1,0:T(8,128)S(1)}, f32[100,128]{1,0:T(8,128)S(1)}, u32[]{:S(2)}, u32[]{:S(2)}) collective-permute-start(f32[100,128]{1,0:T(8,128)S(1)} %slice_select_fusion.2), channel_id=1, source_target_pairs={{0,128},{32,160},{64,192},{96,224},{128,0},{160,32},{192,64},{224,... | collective-permute-start | bytes 153608 | tf_op jit(solution)/shard_map/ppermute | solution.py:83
  70.5 3.2 %collective-permute-done.8 = f32[100,128]{1,0:T(8,128)S(1)} collective-permute-done((f32[100,128]{1,0:T(8,128)S(1)}, f32[100,128]{1,0:T(8,128)S(1)}, u32[]{:S(2)}, u32[]{:S(2)}) %collective-permute-start.8) | collective-permute-done | bytes 51232 | tf_op jit(solution)/shard_map/ppermute | solution.py:83
  73.7 1.1 collective-permute-start.9
  74.9 9.5 %collective-permute-done.9 = f32[100,128]{1,0:T(8,128)S(1)} collective-permute-done((f32[100,128]{1,0:T(8,128)S(1)}, f32[100,128]{1,0:T(8,128)S(1)}, u32[]{:S(2)}, u32[]{:S(2)}) %collective-permute-start.9) | collective-permute-done | bytes 51232 | tf_op jit(solution)/shard_map/ppermute | solution.py:85
  84.5 2.1 %collective-permute-start.3 = (f32[516,128]{1,0:T(8,128)S(1)}, f32[516,128]{1,0:T(8,128)S(1)}, u32[]{:S(2)}, u32[]{:S(2)}) collective-permute-start(f32[516,128]{1,0:T(8,128)S(1)} %pad_maximum_fusion.11), channel_id=1, source_target_pairs={{224,0},{0,32},{32,64},{64,96},{96,128},{128,160},{160,192},{192,2... | collective-permute-start | bytes 792584 | tf_op jit(solution)/shard_map/ppermute | solution.py:15
  86.6 0.8 collective-permute-done.10
  87.8 4.2 %collective-permute-done.11 = f32[100,128]{1,0:T(8,128)S(1)} collective-permute-done((f32[100,128]{1,0:T(8,128)S(1)}, f32[100,128]{1,0:T(8,128)S(1)}, u32[]{:S(2)}, u32[]{:S(2)}) %collective-permute-start.11) | collective-permute-done | bytes 51232 | tf_op jit(solution)/shard_map/ppermute | solution.py:85
  92.0 1.2 %collective-permute-start.12 = (f32[100,128]{1,0:T(8,128)S(1)}, f32[100,128]{1,0:T(8,128)S(1)}, u32[]{:S(2)}, u32[]{:S(2)}) collective-permute-start(f32[100,128]{1,0:T(8,128)S(1)} %add.211), channel_id=1, source_target_pairs={{0,8},{8,0},{16,24},{24,16},{1,9},{9,1},{17,25},{25,17},{2,10},{10... | collective-permute-start | bytes 153608 | tf_op jit(solution)/shard_map/ppermute | solution.py:85
  93.6 2.4 %collective-permute-done.12 = f32[100,128]{1,0:T(8,128)S(1)} collective-permute-done((f32[100,128]{1,0:T(8,128)S(1)}, f32[100,128]{1,0:T(8,128)S(1)}, u32[]{:S(2)}, u32[]{:S(2)}) %collective-permute-start.12) | collective-permute-done | bytes 51232 | tf_op jit(solution)/shard_map/ppermute | solution.py:85
  96.0 3.7 %collective-permute-start.13 = (f32[100,128]{1,0:T(8,128)S(1)}, f32[100,128]{1,0:T(8,128)S(1)}, u32[]{:S(2)}, u32[]{:S(2)}) collective-permute-start(f32[100,128]{1,0:T(8,128)S(1)} %add.212), channel_id=1, source_target_pairs={{0,24},{8,16},{16,8},{24,0},{1,25},{9,17},{17,9},{25,1},{2,26},{10... | collective-permute-start | bytes 153608 | tf_op jit(solution)/shard_map/ppermute | solution.py:85
  99.8 1.4 %collective-permute-done.13 = f32[100,128]{1,0:T(8,128)S(1)} collective-permute-done((f32[100,128]{1,0:T(8,128)S(1)}, f32[100,128]{1,0:T(8,128)S(1)}, u32[]{:S(2)}, u32[]{:S(2)}) %collective-permute-start.13) | collective-permute-done | bytes 51232 | tf_op jit(solution)/shard_map/ppermute | solution.py:85
  101.2 1.3 %collective-permute-start.14 = (f32[100,128]{1,0:T(8,128)S(1)}, f32[100,128]{1,0:T(8,128)S(1)}, u32[]{:S(2)}, u32[]{:S(2)}) collective-permute-start(f32[100,128]{1,0:T(8,128)S(1)} %add.213), channel_id=1, source_target_pairs={{0,128},{32,160},{64,192},{96,224},{128,0},{160,32},{192,64},{224,... | collective-permute-start | bytes 153608 | tf_op jit(solution)/shard_map/ppermute | solution.py:88
  103.8 2.0 %collective-permute-done.14 = f32[100,128]{1,0:T(8,128)S(1)} collective-permute-done((f32[100,128]{1,0:T(8,128)S(1)}, f32[100,128]{1,0:T(8,128)S(1)}, u32[]{:S(2)}, u32[]{:S(2)}) %collective-permute-start.14) | collective-permute-done | bytes 51232 | tf_op jit(solution)/shard_map/ppermute | solution.py:88
  106.7 2.8 %collective-permute-done.15 = f32[200,128]{1,0:T(8,128)S(1)} collective-permute-done((f32[200,128]{1,0:T(8,128)S(1)}, f32[200,128]{1,0:T(8,128)S(1)}, u32[]{:S(2)}, u32[]{:S(2)}) %collective-permute-start.15) | collective-permute-done | bytes 102432 | tf_op jit(solution)/shard_map/ppermute | solution.py:88
  109.5 9.0 %collective-permute-start.16 = (f32[400,128]{1,0:T(8,128)S(1)}, f32[400,128]{1,0:T(8,128)S(1)}, u32[]{:S(2)}, u32[]{:S(2)}) collective-permute-start(f32[400,128]{1,0:T(8,128)S(1)} %maximum_select_fusion), channel_id=1, source_target_pairs={{0,32},{32,0},{64,96},{96,64},{128,160},{160,128},{192,224},{224,1... | collective-permute-start | bytes 614408 | tf_op jit(solution)/shard_map/ppermute | solution.py:88
  119.6 0.8 fusion.53
  (187 shorter events, 25.5 us)
Async XLA Ops:
  0.6 37.1 %copy-start = (f32[128,128]{1,0:T(8,128)S(1)}, f32[128,128]{1,0:T(8,128)}, u32[]{:S(2)}) copy-start(f32[128,128]{1,0:T(8,128)} %param.33) | copy-start | bytes 196612
  4.5 24.3 %collective-permute-start.2 = (f32[517,128]{1,0:T(8,128)S(1)}, f32[517,128]{1,0:T(8,128)S(1)}, u32[]{:S(2)}, u32[]{:S(2)}) collective-permute-start(f32[517,128]{1,0:T(8,128)S(1)} %concatenate.80), channel_id=1, source_target_pairs={{1,0},{2,1},{3,2},{4,3},{5,4},{6,5},{7,6},{0,7},{9,8},{10,9},{11,1... | collective-permute-start | bytes 794120 | tf_op jit(solution)/shard_map/ppermute | solution.py:15
  4.5 24.8 %collective-permute-start.1 = (f32[517,128]{1,0:T(8,128)S(1)}, f32[517,128]{1,0:T(8,128)S(1)}, u32[]{:S(2)}, u32[]{:S(2)}) collective-permute-start(f32[517,128]{1,0:T(8,128)S(1)} %concatenate.80), channel_id=1, source_target_pairs={{8,0},{16,8},{24,16},{0,24},{9,1},{17,9},{25,17},{1,25},{10,2},{18... | collective-permute-start | bytes 794120 | tf_op jit(solution)/shard_map/ppermute | solution.py:15
  10.3 19.4 %collective-permute-start = (f32[517,128]{1,0:T(8,128)S(1)}, f32[517,128]{1,0:T(8,128)S(1)}, u32[]{:S(2)}, u32[]{:S(2)}) collective-permute-start(f32[517,128]{1,0:T(8,128)S(1)} %concatenate.80), channel_id=1, source_target_pairs={{32,0},{64,32},{96,64},{128,96},{160,128},{192,160},{224,192},{0,2... | collective-permute-start | bytes 794120 | tf_op jit(solution)/shard_map/ppermute | solution.py:15
  26.4 1.6 %copy-start.7 = (f32[1,1,1,3,128,128]{5,4,3,2,1,0:T(8,128)S(1)}, f32[1,1,1,3,128,128]{5,4,3,2,1,0:T(8,128)}, u32[]{:S(2)}) copy-start(f32[1,1,1,3,128,128]{5,4,3,2,1,0:T(8,128)} %param.19) | copy-start | bytes 589828
  26.5 2.5 %copy-start.18 = (f32[2,8,128]{2,1,0:T(8,128)S(1)}, f32[2,8,128]{2,1,0:T(8,128)}, u32[]{:S(2)}) copy-start(f32[2,8,128]{2,1,0:T(8,128)} %param.30) | copy-start | bytes 24580
  26.5 3.6 %copy-start.21 = (f32[1,1,1,3,128]{4,2,3,1,0:T(1,128)S(1)}, f32[1,1,1,3,128]{4,2,3,1,0:T(1,128)}, u32[]{:S(2)}) copy-start(f32[1,1,1,3,128]{4,2,3,1,0:T(1,128)} %param.20) | copy-start | bytes 4612
  26.7 4.6 %copy-start.1 = (f32[128,128]{1,0:T(8,128)S(1)}, f32[128,128]{1,0:T(8,128)}, u32[]{:S(2)}) copy-start(f32[128,128]{1,0:T(8,128)} %param.28) | copy-start | bytes 196612
  29.7 3.5 %copy-start.16 = (f32[517,128]{1,0:T(8,128)}, f32[517,128]{1,0:T(8,128)S(1)}, u32[]{:S(2)}) copy-start(f32[517,128]{1,0:T(8,128)S(1)} %collective-permute-done) | copy-start | bytes 794116
  33.0 0.7 copy-start.19
  33.7 0.8 copy-start.23
  34.5 9.3 %copy-start.11 = (f32[128,1792]{1,0:T(8,128)}, f32[128,1792]{1,0:T(8,128)S(1)}, u32[]{:S(2)}) copy-start(f32[128,1792]{1,0:T(8,128)S(1)} %fusion.7) | copy-start | bytes 2752516
  34.5 1.0 copy-start.15
  35.5 8.4 %copy-start.25 = (f32[128,1792]{1,0:T(8,128)}, f32[128,1792]{1,0:T(8,128)S(1)}, u32[]{:S(2)}) copy-start(f32[128,1792]{1,0:T(8,128)S(1)} %get-tuple-element.61) | copy-start | bytes 2752516
  36.9 1.4 %copy-start.22 = (f32[128]{0:T(128)S(1)}, f32[128]{0:T(128)}, u32[]{:S(2)}) copy-start(f32[128]{0:T(128)} %param.34) | copy-start | bytes 1540
  37.7 1.4 %copy-start.2 = (f32[128,1792]{1,0:T(8,128)}, f32[128,1792]{1,0:T(8,128)S(1)}, u32[]{:S(2)}) copy-start(f32[128,1792]{1,0:T(8,128)S(1)} %get-tuple-element.13) | copy-start | bytes 2752516
  38.3 3.0 %copy-start.4 = (f32[128,1792]{1,0:T(8,128)}, f32[128,1792]{1,0:T(8,128)S(1)}, u32[]{:S(2)}) copy-start(f32[128,1792]{1,0:T(8,128)S(1)} %convolution_bitcast_fusion.4) | copy-start | bytes 2752516
  43.8 1.2 copy-start.13
  45.4 2.2 %copy-start.6 = (f32[128,1792]{1,0:T(8,128)S(1)}, f32[128,1792]{1,0:T(8,128)}, u32[]{:S(2)}) copy-start(f32[128,1792]{1,0:T(8,128)} %get-tuple-element.17) | copy-start | bytes 2752516
  48.8 1.2 copy-start.20
  48.8 1.3 %copy-start.17 = (f32[128,128]{1,0:T(8,128)S(1)}, f32[128,128]{1,0:T(8,128)}, u32[]{:S(2)}) copy-start(f32[128,128]{1,0:T(8,128)} %param.27) | copy-start | bytes 196612
  50.0 1.3 %copy-start.10 = (f32[1,1,1,128,128]{4,3,2,1,0:T(8,128)S(1)}, f32[1,1,1,128,128]{4,3,2,1,0:T(8,128)}, u32[]{:S(2)}) copy-start(f32[1,1,1,128,128]{4,3,2,1,0:T(8,128)} %param.18) | copy-start | bytes 196612
  52.0 5.3 %copy-start.8 = (f32[515,128]{1,0:T(8,128)}, f32[515,128]{1,0:T(8,128)S(1)}, u32[]{:S(2)}) copy-start(f32[515,128]{1,0:T(8,128)S(1)} %convolution_add_fusion.2) | copy-start | bytes 791044
  52.7 1.3 %copy-start.5 = (f32[128,1792]{1,0:T(8,128)S(1)}, f32[128,1792]{1,0:T(8,128)}, u32[]{:S(2)}) copy-start(f32[128,1792]{1,0:T(8,128)} %copy-done.4) | copy-start | bytes 2752516
  53.4 4.9 %copy-start.9 = (f32[515,128]{1,0:T(8,128)}, f32[515,128]{1,0:T(8,128)S(1)}, u32[]{:S(2)}) copy-start(f32[515,128]{1,0:T(8,128)S(1)} %convolution_add_fusion.1) | copy-start | bytes 791044
  54.1 5.3 %copy-start.12 = (f32[128,1792]{1,0:T(8,128)S(1)}, f32[128,1792]{1,0:T(8,128)}, u32[]{:S(2)}) copy-start(f32[128,1792]{1,0:T(8,128)} %copy-done.11) | copy-start | bytes 2752516
  54.1 5.3 %copy-start.14 = (f32[128,1792]{1,0:T(8,128)S(1)}, f32[128,1792]{1,0:T(8,128)}, u32[]{:S(2)}) copy-start(f32[128,1792]{1,0:T(8,128)} %copy-done.13) | copy-start | bytes 2752516
  54.1 5.3 %copy-start.26 = (f32[128,1792]{1,0:T(8,128)S(1)}, f32[128,1792]{1,0:T(8,128)}, u32[]{:S(2)}) copy-start(f32[128,1792]{1,0:T(8,128)} %copy-done.25) | copy-start | bytes 2752516
  55.3 44.4 %collective-permute-start.5 = (f32[516,128]{1,0:T(8,128)S(1)}, f32[516,128]{1,0:T(8,128)S(1)}, u32[]{:S(2)}, u32[]{:S(2)}) collective-permute-start(f32[516,128]{1,0:T(8,128)S(1)} %pad_maximum_fusion.13), channel_id=1, source_target_pairs={{7,0},{0,1},{1,2},{2,3},{3,4},{4,5},{5,6},{6,7},{15,8},{8,9},{9,10... | collective-permute-start | bytes 792584 | tf_op jit(solution)/shard_map/ppermute | solution.py:15
  59.4 1.2 copy-start.3
  60.6 4.5 %slice-start.1 = ((f32[515,128]{1,0:T(8,128)}), f32[387,128]{1,0:T(8,128)S(1)}, s32[]{:S(2)}) async-start(f32[515,128]{1,0:T(8,128)} %copy-done.9), calls=%async_computation.1 | async-start | bytes 401408 | tf_op jit(solution)/shard_map/transpose(jvp())/split | solution.py:187
  61.4 13.4 %slice-start = ((f32[515,128]{1,0:T(8,128)}), f32[387,128]{1,0:T(8,128)S(1)}, s32[]{:S(2)}) async-start(f32[515,128]{1,0:T(8,128)} %copy-done.8), calls=%async_computation | async-start | bytes 401408 | tf_op jit(solution)/shard_map/transpose(jvp())/split | solution.py:187
  61.5 3.3 %collective-permute-start.6 = (f32[400,128]{1,0:T(8,128)S(1)}, f32[400,128]{1,0:T(8,128)S(1)}, u32[]{:S(2)}, u32[]{:S(2)}) collective-permute-start(f32[400,128]{1,0:T(8,128)S(1)} %slice_select_fusion), channel_id=1, source_target_pairs={{0,32},{32,0},{64,96},{96,64},{128,160},{160,128},{192,224},{224,1... | collective-permute-start | bytes 614408 | tf_op jit(solution)/shard_map/ppermute | solution.py:83
  64.9 4.2 %collective-permute-start.7 = (f32[200,128]{1,0:T(8,128)S(1)}, f32[200,128]{1,0:T(8,128)S(1)}, u32[]{:S(2)}, u32[]{:S(2)}) collective-permute-start(f32[200,128]{1,0:T(8,128)S(1)} %slice_select_fusion.1), channel_id=1, source_target_pairs={{0,64},{32,96},{64,0},{96,32},{128,192},{160,224},{192,128},{224,1... | collective-permute-start | bytes 307208 | tf_op jit(solution)/shard_map/ppermute | solution.py:83
  69.1 4.6 %collective-permute-start.8 = (f32[100,128]{1,0:T(8,128)S(1)}, f32[100,128]{1,0:T(8,128)S(1)}, u32[]{:S(2)}, u32[]{:S(2)}) collective-permute-start(f32[100,128]{1,0:T(8,128)S(1)} %slice_select_fusion.2), channel_id=1, source_target_pairs={{0,128},{32,160},{64,192},{96,224},{128,0},{160,32},{192,64},{224,... | collective-permute-start | bytes 153608 | tf_op jit(solution)/shard_map/ppermute | solution.py:83
  70.4 35.6 %copy-start.24 = (f32[8]{0:T(128)S(1)}, f32[8]{0:T(128)}, u32[]{:S(2)}) copy-start(f32[8]{0:T(128)} %param.35) | copy-start | bytes 100
  70.4 29.3 %collective-permute-start.4 = (f32[516,128]{1,0:T(8,128)S(1)}, f32[516,128]{1,0:T(8,128)S(1)}, u32[]{:S(2)}, u32[]{:S(2)}) collective-permute-start(f32[516,128]{1,0:T(8,128)S(1)} %pad_maximum_fusion.12), channel_id=1, source_target_pairs={{24,0},{0,8},{8,16},{16,24},{25,1},{1,9},{9,17},{17,25},{26,2},{2,... | collective-permute-start | bytes 792584 | tf_op jit(solution)/shard_map/ppermute | solution.py:15
  73.7 10.6 %collective-permute-start.9 = (f32[100,128]{1,0:T(8,128)S(1)}, f32[100,128]{1,0:T(8,128)S(1)}, u32[]{:S(2)}, u32[]{:S(2)}) collective-permute-start(f32[100,128]{1,0:T(8,128)S(1)} %select_add_fusion.2), channel_id=1, source_target_pairs={{0,1},{1,0},{2,3},{3,2},{4,5},{5,4},{6,7},{7,6},{8,9},{9,8},{10,11... | collective-permute-start | bytes 153608 | tf_op jit(solution)/shard_map/ppermute | solution.py:85
  84.3 3.1 %collective-permute-start.10 = (f32[100,128]{1,0:T(8,128)S(1)}, f32[100,128]{1,0:T(8,128)S(1)}, u32[]{:S(2)}, u32[]{:S(2)}) collective-permute-start(f32[100,128]{1,0:T(8,128)S(1)} %add.209), channel_id=1, source_target_pairs={{0,2},{1,3},{2,0},{3,1},{4,6},{5,7},{6,4},{7,5},{8,10},{9,11},{10,... | collective-permute-start | bytes 153608 | tf_op jit(solution)/shard_map/ppermute | solution.py:85
  84.5 15.2 %collective-permute-start.3 = (f32[516,128]{1,0:T(8,128)S(1)}, f32[516,128]{1,0:T(8,128)S(1)}, u32[]{:S(2)}, u32[]{:S(2)}) collective-permute-start(f32[516,128]{1,0:T(8,128)S(1)} %pad_maximum_fusion.11), channel_id=1, source_target_pairs={{224,0},{0,32},{32,64},{64,96},{96,128},{128,160},{160,192},{192,2... | collective-permute-start | bytes 792584 | tf_op jit(solution)/shard_map/ppermute | solution.py:15
  87.4 4.6 %collective-permute-start.11 = (f32[100,128]{1,0:T(8,128)S(1)}, f32[100,128]{1,0:T(8,128)S(1)}, u32[]{:S(2)}, u32[]{:S(2)}) collective-permute-start(f32[100,128]{1,0:T(8,128)S(1)} %add.210), channel_id=1, source_target_pairs={{0,6},{1,7},{2,4},{3,5},{4,2},{5,3},{6,0},{7,1},{8,14},{9,15},{10,... | collective-permute-start | bytes 153608 | tf_op jit(solution)/shard_map/ppermute | solution.py:85
  92.0 4.0 %collective-permute-start.12 = (f32[100,128]{1,0:T(8,128)S(1)}, f32[100,128]{1,0:T(8,128)S(1)}, u32[]{:S(2)}, u32[]{:S(2)}) collective-permute-start(f32[100,128]{1,0:T(8,128)S(1)} %add.211), channel_id=1, source_target_pairs={{0,8},{8,0},{16,24},{24,16},{1,9},{9,1},{17,25},{25,17},{2,10},{10... | collective-permute-start | bytes 153608 | tf_op jit(solution)/shard_map/ppermute | solution.py:85
  96.0 5.2 %collective-permute-start.13 = (f32[100,128]{1,0:T(8,128)S(1)}, f32[100,128]{1,0:T(8,128)S(1)}, u32[]{:S(2)}, u32[]{:S(2)}) collective-permute-start(f32[100,128]{1,0:T(8,128)S(1)} %add.212), channel_id=1, source_target_pairs={{0,24},{8,16},{16,8},{24,0},{1,25},{9,17},{17,9},{25,1},{2,26},{10... | collective-permute-start | bytes 153608 | tf_op jit(solution)/shard_map/ppermute | solution.py:85
  101.2 4.6 %collective-permute-start.14 = (f32[100,128]{1,0:T(8,128)S(1)}, f32[100,128]{1,0:T(8,128)S(1)}, u32[]{:S(2)}, u32[]{:S(2)}) collective-permute-start(f32[100,128]{1,0:T(8,128)S(1)} %add.213), channel_id=1, source_target_pairs={{0,128},{32,160},{64,192},{96,224},{128,0},{160,32},{192,64},{224,... | collective-permute-start | bytes 153608 | tf_op jit(solution)/shard_map/ppermute | solution.py:88
  105.8 3.6 %collective-permute-start.15 = (f32[200,128]{1,0:T(8,128)S(1)}, f32[200,128]{1,0:T(8,128)S(1)}, u32[]{:S(2)}, u32[]{:S(2)}) collective-permute-start(f32[200,128]{1,0:T(8,128)S(1)} %maximum_select_fusion.1), channel_id=1, source_target_pairs={{0,64},{32,96},{64,0},{96,32},{128,192},{160,224},{192,128},{224,1... | collective-permute-start | bytes 307208 | tf_op jit(solution)/shard_map/ppermute | solution.py:88
  109.5 10.1 %collective-permute-start.16 = (f32[400,128]{1,0:T(8,128)S(1)}, f32[400,128]{1,0:T(8,128)S(1)}, u32[]{:S(2)}, u32[]{:S(2)}) collective-permute-start(f32[400,128]{1,0:T(8,128)S(1)} %maximum_select_fusion), channel_id=1, source_target_pairs={{0,32},{32,0},{64,96},{96,64},{128,160},{160,128},{192,224},{224,1... | collective-permute-start | bytes 614408 | tf_op jit(solution)/shard_map/ppermute | solution.py:88

commit v3 on v2

--- a/solution.py
+++ b/solution.py
@@ -68,24 +68,34 @@
     return index ^ distance
 
 
+def halving_order(steps):
+    ordered = list(steps)
+    for k in range(len(ordered) - 1):
+        axis, distance, size = ordered[k + 1]
+        if ordered[k] == (axis, distance // 2, size) and distance >= 4 and 2 * distance == size:
+            ordered[k], ordered[k + 1] = ordered[k + 1], ordered[k]
+    return ordered
+
+
 def sum_over_devices(rows):
     steps = halving_steps()
     if any(size & (size - 1) for _, _, size in steps):
         return lax.psum(rows, ("gx", "gy", "gz"))
     halvings = min(halving_count, len(steps))
     padded = jnp.pad(rows, ((0, (-rows.shape[0]) % (2**halvings)), (0, 0)))
-    for axis, distance, size in steps[:halvings]:
+    halving = halving_order(steps[:halvings])
+    for axis, distance, size in halving:
         upper = (lax.axis_index(axis) // distance) % 2 == 1
         half = padded.shape[0] // 2
         low, high = padded[:half], padded[half:]
         keep = jnp.where(upper, high, low)
         send = jnp.where(upper, low, high)
-        padded = keep + lax.ppermute(send, axis, [(i, i ^ distance) for i in range(size)])
+        padded = keep + lax.ppermute(send, axis, [(i, exchange_partner(i, distance, size)) for i in range(size)])
     for axis, distance, size in steps[halvings:]:
         padded = padded + lax.ppermute(padded, axis, [(i, exchange_partner(i, distance, size)) for i in range(size)])
-    for axis, distance, size in reversed(steps[:halvings]):
+    for axis, distance, size in reversed(halving):
         upper = (lax.axis_index(axis) // distance) % 2 == 1
-        other = lax.ppermute(padded, axis, [(i, i ^ distance) for i in range(size)])
+        other = lax.ppermute(padded, axis, [(i, exchange_partner(i, distance, size)) for i in range(size)])
         padded = jnp.where(
             upper, jnp.concatenate([other, padded]), jnp.concatenate([padded, other])
         )

time: 121 us -> 119 us (0.983)
  waiting for transfers between devices: 31.7 us -> 26.2 us
  starting transfers between devices: 31.6 us -> 34.8 us
    ppermute x6 -> x3, starting transfers between devices: 14.1 us -> 3.37 us  [sum_over_devices(): lax.ppermute(send, axis, [(i, exchange_partner(i, distance, size)) for i...]
    ppermute x5 -> x8, starting transfers between devices: 6.23 us -> 16.9 us  [sum_over_devices(): lax.ppermute(padded, axis, [(i, exchange_partner(i, distance, size)) for...]
    ppermute x6 -> x3, waiting for transfers between devices: 13.4 us -> 8.1 us  [sum_over_devices(): lax.ppermute(send, axis, [(i, exchange_partner(i, distance, size)) for i...]
    ppermute x6, starting transfers between devices: 11.2 us -> 14.6 us  [from_behind(): return lax.ppermute(block, axis, route)]
    ppermute x5 -> x8, waiting for transfers between devices: 18.3 us -> 18.1 us  [sum_over_devices(): lax.ppermute(padded, axis, [(i, exchange_partner(i, distance, size)) for...]
  transfers between devices with their start and end apart: 17 -> 17, of which waited for: 11 -> 10; matrix products, arithmetic and copies ran while one was open for 21% -> 21% of each run, Pallas kernels for 0% -> 0%
where the time goes in v3:
time: 119 us; the launch traced here: 118 us
  matrix products  37.6 us (32%)
  starting transfers between devices  34.8 us (29%)
  waiting for transfers between devices  26.2 us (22%)
  local copies, waits for them, and re-layouts  9.62 us (8%)
  other arithmetic  7.6 us (6%)
  between operations  2.33 us (2%)
    ppermute x8, waiting for transfers between devices, sum_over_devices(): lax.ppermute(padded, axis, [(i, exchange_partner(i, distance, size)) for...  18.1 us
    ppermute x8, starting transfers between devices, sum_over_devices(): lax.ppermute(padded, axis, [(i, exchange_partner(i, distance, size)) for...  16.9 us
    ppermute x6, starting transfers between devices, from_behind(): return lax.ppermute(block, axis, route)  14.6 us
    ppermute x3, waiting for transfers between devices, sum_over_devices(): lax.ppermute(send, axis, [(i, exchange_partner(i, distance, size)) for i...  8.1 us
    dot_general x15, matrix products, projected(): jnp.dot(matrix.T, table[:channels], precision=lax.Precision.HIGH)  6.07 us
    dot_general x3, matrix products, edge_energy(): jnp.dot(read_weight.T, mixed_latent, precision=lax.Precision.HIGH)  3.65 us
    ppermute x3, starting transfers between devices, sum_over_devices(): lax.ppermute(send, axis, [(i, exchange_partner(i, distance, size)) for i...  3.37 us
    dot_general x10, matrix products, projected(): jnp.dot(embed_row.T, hot_kinds, precision=highest)  3.36 us
  transfers between devices with their start and end apart: 17, of which 10 were waited for; matrix products, arithmetic and copies ran while one was open for 21% of the time, Pallas kernels for 0%

profile of v3, /device:TPU:33, one launch (start us, length us, event | category | flops | bytes accessed | tf_op | source)
XLA Modules:
  0.0 118.2 jit_solution(15218704486780699430)
XLA Ops:
  2.0 2.5 %concatenate.80 = f32[517,128]{1,0:T(8,128)S(1)} concatenate(f32[128,128]{1,0:T(8,128)} %bitcast.328, f32[384,128]{1,0:T(8,128)} %bitcast.325, f32[3,128]{1,0:T(4,128)S(1)} %bitcast.338, f32[1,128]{1,0:T(1,128)} %bitcast.382, f32[1,128]{1,0:T(1,128)S(1)} %convert_bitcast_fusion), dimensions={0} | concatenate | bytes 529408 | tf_op jit(solution)/shard_map/concatenate | solution.py:153
  4.5 5.8 %collective-permute-start.1 = (f32[517,128]{1,0:T(8,128)S(1)}, f32[517,128]{1,0:T(8,128)S(1)}, u32[]{:S(2)}, u32[]{:S(2)}) collective-permute-start(f32[517,128]{1,0:T(8,128)S(1)} %concatenate.80), channel_id=1, source_target_pairs={{8,0},{16,8},{24,16},{0,24},{9,1},{17,9},{25,17},{1,25},{10,2},{18... | collective-permute-start | bytes 794120 | tf_op jit(solution)/shard_map/ppermute | solution.py:15
  10.3 1.2 %collective-permute-start = (f32[517,128]{1,0:T(8,128)S(1)}, f32[517,128]{1,0:T(8,128)S(1)}, u32[]{:S(2)}, u32[]{:S(2)}) collective-permute-start(f32[517,128]{1,0:T(8,128)S(1)} %concatenate.80), channel_id=1, source_target_pairs={{32,0},{64,32},{96,64},{128,96},{160,128},{192,160},{224,192},{0,2... | collective-permute-start | bytes 794120 | tf_op jit(solution)/shard_map/ppermute | solution.py:15
  11.6 0.8 fusion.236
  12.4 0.9 fusion.43
  13.3 0.9 convolution_bitcast_fusion.22
  14.9 1.4 %fusion.238 = (s32[1,1,1,1]{3,2,1,0:T(1,128)}, s32[1,1,1,1]{3,2,1,0:T(1,128)}, s32[1,1,1,1]{3,2,1,0:T(1,128)}, s32[1,1,1,1]{3,2,1,0:T(1,128)}) fusion(s32[1,1,1,4]{3,2,1,0:T(1,128)} %param.26), kind=kLoop, calls=%fused_computation.384 | loop fusion | bytes 32 | tf_op jit(solution)/shard_map/slice | solution.py:171
  17.6 0.8 fusion.237
  18.4 1.0 convolution_reduce_fusion
  19.4 1.1 fusion.216
  20.5 1.1 fusion.214
  21.6 0.8 convolution_bitcast_fusion.30
  22.4 1.0 fusion.17
  23.4 1.0 fusion.16
  24.4 2.1 %fusion.35 = f32[515,1792]{1,0:T(8,128)S(1)} fusion(s32[1792]{0:T(1024)S(1)} %pad_add_fusion.12, f32[3,128]{1,0:T(4,128)S(1)} %bitcast.339, f32[384,128]{1,0:T(8,128)} %bitcast.326, f32[128,128]{1,0:T(8,128)S(1)} %fusion.17), kind=kOutput, calls=%fused_computation.113 | convolution fusion | flops 709133056 | bytes 3962368 | tf_op jit(solution)/shard_map/jvp()/dot_general | solution.py:204
  26.7 1.3 %iota_compare_fusion.52 = (pred[256]{0:T(512)(128)(4,1)S(1)}, pred[256]{0:T(512)(128)(4,1)S(1)}) fusion(s32[]{:T(128)} %bitcast.12, s32[]{:T(128)} %bitcast.11), kind=kLoop, calls=%fused_computation.331 | loop fusion | flops 512 | bytes 520 | tf_op jit(solution)/shard_map/lt | solution.py:171
  34.5 1.0 multiply_add_fusion.2
  36.1 0.8 multiply_reduce_fusion.4
  36.9 0.8 multiply_add_fusion.1
  38.3 0.8 convolution_reduce_fusion.1
  39.1 2.2 %multiply_reduce_fusion.5 = (f32[1792]{0:T(1024)S(1)}, f32[128,1792]{1,0:T(8,128)S(1)}, f32[128,1792]{1,0:T(8,128)}, f32[128,1792]{1,0:T(8,128)S(1)}, f32[128,1792]{1,0:T(8,128)S(1)}) fusion(f32[128,1792]{1,0:T(8,128)S(1)} %get-tuple-element.11, f32[128,1792]{1,0:T(8,128)S(1)} %get-tuple-element.62, f32[128,1792]{1,0:T(8,128)S(1)} %get-tuple-element.12, ...), kind=kOutput, calls=%fused_computation.101 | convolution fusion | flops 180746496 | bytes 9262592 | tf_op jit(solution)/shard_map/transpose(jvp())/dot_general | solution.py:41
  43.9 1.1 fusion.31
  45.4 0.8 multiply_reduce_fusion
  47.6 1.2 fusion.3
  48.8 1.2 fusion.15
  54.1 0.9 convolution_bitcast_fusion.28
  55.3 1.9 %collective-permute-start.5 = (f32[516,128]{1,0:T(8,128)S(1)}, f32[516,128]{1,0:T(8,128)S(1)}, u32[]{:S(2)}, u32[]{:S(2)}) collective-permute-start(f32[516,128]{1,0:T(8,128)S(1)} %pad_maximum_fusion.13), channel_id=1, source_target_pairs={{7,0},{0,1},{1,2},{2,3},{3,4},{4,5},{5,6},{6,7},{15,8},{8,9},{9,10... | collective-permute-start | bytes 792584 | tf_op jit(solution)/shard_map/ppermute | solution.py:15
  57.3 1.0 fusion.119
  59.4 1.0 constant_dynamic-update-slice_fusion.2
  60.6 0.9 convolution_dynamic-update-slice_fusion
  61.5 2.3 %collective-permute-start.6 = (f32[400,128]{1,0:T(8,128)S(1)}, f32[400,128]{1,0:T(8,128)S(1)}, u32[]{:S(2)}, u32[]{:S(2)}) collective-permute-start(f32[400,128]{1,0:T(8,128)S(1)} %slice_select_fusion), channel_id=1, source_target_pairs={{0,32},{32,0},{64,96},{96,64},{128,160},{160,128},{192,224},{224,1... | collective-permute-start | bytes 614408 | tf_op jit(solution)/shard_map/ppermute | solution.py:93
  63.9 0.9 collective-permute-done.6
  64.9 1.0 collective-permute-start.7
  66.0 4.3 %collective-permute-done.7 = f32[200,128]{1,0:T(8,128)S(1)} collective-permute-done((f32[200,128]{1,0:T(8,128)S(1)}, f32[200,128]{1,0:T(8,128)S(1)}, u32[]{:S(2)}, u32[]{:S(2)}) %collective-permute-start.7) | collective-permute-done | bytes 102432 | tf_op jit(solution)/shard_map/ppermute | solution.py:93
  70.6 2.8 %collective-permute-done.8 = f32[100,128]{1,0:T(8,128)S(1)} collective-permute-done((f32[100,128]{1,0:T(8,128)S(1)}, f32[100,128]{1,0:T(8,128)S(1)}, u32[]{:S(2)}, u32[]{:S(2)}) %collective-permute-start.8) | collective-permute-done | bytes 51232 | tf_op jit(solution)/shard_map/ppermute | solution.py:93
  73.4 1.1 collective-permute-start.9
  74.6 6.2 %collective-permute-done.9 = f32[100,128]{1,0:T(8,128)S(1)} collective-permute-done((f32[100,128]{1,0:T(8,128)S(1)}, f32[100,128]{1,0:T(8,128)S(1)}, u32[]{:S(2)}, u32[]{:S(2)}) %collective-permute-start.9) | collective-permute-done | bytes 51232 | tf_op jit(solution)/shard_map/ppermute | solution.py:95
  80.9 5.5 %collective-permute-start.3 = (f32[516,128]{1,0:T(8,128)S(1)}, f32[516,128]{1,0:T(8,128)S(1)}, u32[]{:S(2)}, u32[]{:S(2)}) collective-permute-start(f32[516,128]{1,0:T(8,128)S(1)} %pad_maximum_fusion.11), channel_id=1, source_target_pairs={{224,0},{0,32},{32,64},{64,96},{96,128},{128,160},{160,192},{192,2... | collective-permute-start | bytes 792584 | tf_op jit(solution)/shard_map/ppermute | solution.py:15
  86.8 4.2 %collective-permute-done.11 = f32[100,128]{1,0:T(8,128)S(1)} collective-permute-done((f32[100,128]{1,0:T(8,128)S(1)}, f32[100,128]{1,0:T(8,128)S(1)}, u32[]{:S(2)}, u32[]{:S(2)}) %collective-permute-start.11) | collective-permute-done | bytes 51232 | tf_op jit(solution)/shard_map/ppermute | solution.py:95
  91.0 2.4 %collective-permute-start.12 = (f32[100,128]{1,0:T(8,128)S(1)}, f32[100,128]{1,0:T(8,128)S(1)}, u32[]{:S(2)}, u32[]{:S(2)}) collective-permute-start(f32[100,128]{1,0:T(8,128)S(1)} %add.211), channel_id=1, source_target_pairs={{0,8},{8,0},{16,24},{24,16},{1,9},{9,1},{17,25},{25,17},{2,10},{10... | collective-permute-start | bytes 153608 | tf_op jit(solution)/shard_map/ppermute | solution.py:95
  93.8 1.2 %collective-permute-done.12 = f32[100,128]{1,0:T(8,128)S(1)} collective-permute-done((f32[100,128]{1,0:T(8,128)S(1)}, f32[100,128]{1,0:T(8,128)S(1)}, u32[]{:S(2)}, u32[]{:S(2)}) %collective-permute-start.12) | collective-permute-done | bytes 51232 | tf_op jit(solution)/shard_map/ppermute | solution.py:95
  95.0 4.8 %collective-permute-start.13 = (f32[100,128]{1,0:T(8,128)S(1)}, f32[100,128]{1,0:T(8,128)S(1)}, u32[]{:S(2)}, u32[]{:S(2)}) collective-permute-start(f32[100,128]{1,0:T(8,128)S(1)} %add.212), channel_id=1, source_target_pairs={{0,24},{8,16},{16,8},{24,0},{1,25},{9,17},{17,9},{25,1},{2,26},{10... | collective-permute-start | bytes 153608 | tf_op jit(solution)/shard_map/ppermute | solution.py:95
  99.9 1.4 %collective-permute-done.13 = f32[100,128]{1,0:T(8,128)S(1)} collective-permute-done((f32[100,128]{1,0:T(8,128)S(1)}, f32[100,128]{1,0:T(8,128)S(1)}, u32[]{:S(2)}, u32[]{:S(2)}) %collective-permute-start.13) | collective-permute-done | bytes 51232 | tf_op jit(solution)/shard_map/ppermute | solution.py:95
  101.3 1.0 collective-permute-start.14
  103.5 1.2 collective-permute-done.14
  106.0 3.4 %collective-permute-done.15 = f32[200,128]{1,0:T(8,128)S(1)} collective-permute-done((f32[200,128]{1,0:T(8,128)S(1)}, f32[200,128]{1,0:T(8,128)S(1)}, u32[]{:S(2)}, u32[]{:S(2)}) %collective-permute-start.15) | collective-permute-done | bytes 102432 | tf_op jit(solution)/shard_map/ppermute | solution.py:98
  109.5 6.8 %collective-permute-start.16 = (f32[400,128]{1,0:T(8,128)S(1)}, f32[400,128]{1,0:T(8,128)S(1)}, u32[]{:S(2)}, u32[]{:S(2)}) collective-permute-start(f32[400,128]{1,0:T(8,128)S(1)} %maximum_select_fusion), channel_id=1, source_target_pairs={{0,32},{32,0},{64,96},{96,64},{128,160},{160,128},{192,224},{224,1... | collective-permute-start | bytes 614408 | tf_op jit(solution)/shard_map/ppermute | solution.py:98
  117.4 0.8 fusion.53
  (187 shorter events, 25.3 us)
Async XLA Ops:
  0.6 37.1 %copy-start = (f32[128,128]{1,0:T(8,128)S(1)}, f32[128,128]{1,0:T(8,128)}, u32[]{:S(2)}) copy-start(f32[128,128]{1,0:T(8,128)} %param.33) | copy-start | bytes 196612
  4.5 24.3 %collective-permute-start.2 = (f32[517,128]{1,0:T(8,128)S(1)}, f32[517,128]{1,0:T(8,128)S(1)}, u32[]{:S(2)}, u32[]{:S(2)}) collective-permute-start(f32[517,128]{1,0:T(8,128)S(1)} %concatenate.80), channel_id=1, source_target_pairs={{1,0},{2,1},{3,2},{4,3},{5,4},{6,5},{7,6},{0,7},{9,8},{10,9},{11,1... | collective-permute-start | bytes 794120 | tf_op jit(solution)/shard_map/ppermute | solution.py:15
  4.5 24.8 %collective-permute-start.1 = (f32[517,128]{1,0:T(8,128)S(1)}, f32[517,128]{1,0:T(8,128)S(1)}, u32[]{:S(2)}, u32[]{:S(2)}) collective-permute-start(f32[517,128]{1,0:T(8,128)S(1)} %concatenate.80), channel_id=1, source_target_pairs={{8,0},{16,8},{24,16},{0,24},{9,1},{17,9},{25,17},{1,25},{10,2},{18... | collective-permute-start | bytes 794120 | tf_op jit(solution)/shard_map/ppermute | solution.py:15
  10.3 19.4 %collective-permute-start = (f32[517,128]{1,0:T(8,128)S(1)}, f32[517,128]{1,0:T(8,128)S(1)}, u32[]{:S(2)}, u32[]{:S(2)}) collective-permute-start(f32[517,128]{1,0:T(8,128)S(1)} %concatenate.80), channel_id=1, source_target_pairs={{32,0},{64,32},{96,64},{128,96},{160,128},{192,160},{224,192},{0,2... | collective-permute-start | bytes 794120 | tf_op jit(solution)/shard_map/ppermute | solution.py:15
  26.4 1.6 %copy-start.7 = (f32[1,1,1,3,128,128]{5,4,3,2,1,0:T(8,128)S(1)}, f32[1,1,1,3,128,128]{5,4,3,2,1,0:T(8,128)}, u32[]{:S(2)}) copy-start(f32[1,1,1,3,128,128]{5,4,3,2,1,0:T(8,128)} %param.19) | copy-start | bytes 589828
  26.5 2.5 %copy-start.18 = (f32[2,8,128]{2,1,0:T(8,128)S(1)}, f32[2,8,128]{2,1,0:T(8,128)}, u32[]{:S(2)}) copy-start(f32[2,8,128]{2,1,0:T(8,128)} %param.30) | copy-start | bytes 24580
  26.5 3.6 %copy-start.21 = (f32[1,1,1,3,128]{4,2,3,1,0:T(1,128)S(1)}, f32[1,1,1,3,128]{4,2,3,1,0:T(1,128)}, u32[]{:S(2)}) copy-start(f32[1,1,1,3,128]{4,2,3,1,0:T(1,128)} %param.20) | copy-start | bytes 4612
  26.7 4.6 %copy-start.1 = (f32[128,128]{1,0:T(8,128)S(1)}, f32[128,128]{1,0:T(8,128)}, u32[]{:S(2)}) copy-start(f32[128,128]{1,0:T(8,128)} %param.28) | copy-start | bytes 196612
  29.7 3.5 %copy-start.16 = (f32[517,128]{1,0:T(8,128)}, f32[517,128]{1,0:T(8,128)S(1)}, u32[]{:S(2)}) copy-start(f32[517,128]{1,0:T(8,128)S(1)} %collective-permute-done) | copy-start | bytes 794116
  33.0 0.7 copy-start.19
  33.7 0.8 copy-start.23
  34.5 9.3 %copy-start.11 = (f32[128,1792]{1,0:T(8,128)}, f32[128,1792]{1,0:T(8,128)S(1)}, u32[]{:S(2)}) copy-start(f32[128,1792]{1,0:T(8,128)S(1)} %fusion.7) | copy-start | bytes 2752516
  34.5 1.0 copy-start.15
  35.5 8.4 %copy-start.25 = (f32[128,1792]{1,0:T(8,128)}, f32[128,1792]{1,0:T(8,128)S(1)}, u32[]{:S(2)}) copy-start(f32[128,1792]{1,0:T(8,128)S(1)} %get-tuple-element.61) | copy-start | bytes 2752516
  36.9 1.4 %copy-start.22 = (f32[128]{0:T(128)S(1)}, f32[128]{0:T(128)}, u32[]{:S(2)}) copy-start(f32[128]{0:T(128)} %param.34) | copy-start | bytes 1540
  37.7 1.4 %copy-start.2 = (f32[128,1792]{1,0:T(8,128)}, f32[128,1792]{1,0:T(8,128)S(1)}, u32[]{:S(2)}) copy-start(f32[128,1792]{1,0:T(8,128)S(1)} %get-tuple-element.13) | copy-start | bytes 2752516
  38.3 3.0 %copy-start.4 = (f32[128,1792]{1,0:T(8,128)}, f32[128,1792]{1,0:T(8,128)S(1)}, u32[]{:S(2)}) copy-start(f32[128,1792]{1,0:T(8,128)S(1)} %convolution_bitcast_fusion.4) | copy-start | bytes 2752516
  43.8 1.2 copy-start.13
  45.4 2.2 %copy-start.6 = (f32[128,1792]{1,0:T(8,128)S(1)}, f32[128,1792]{1,0:T(8,128)}, u32[]{:S(2)}) copy-start(f32[128,1792]{1,0:T(8,128)} %get-tuple-element.17) | copy-start | bytes 2752516
  48.8 1.2 %copy-start.20 = (s32[1,1,1,128]{3,2,1,0:T(1,128)S(1)}, s32[1,1,1,128]{3,2,1,0:T(1,128)}, u32[]{:S(2)}) copy-start(s32[1,1,1,128]{3,2,1,0:T(1,128)} %param.21) | copy-start | bytes 1540
  48.8 1.3 %copy-start.17 = (f32[128,128]{1,0:T(8,128)S(1)}, f32[128,128]{1,0:T(8,128)}, u32[]{:S(2)}) copy-start(f32[128,128]{1,0:T(8,128)} %param.27) | copy-start | bytes 196612
  50.0 1.3 %copy-start.10 = (f32[1,1,1,128,128]{4,3,2,1,0:T(8,128)S(1)}, f32[1,1,1,128,128]{4,3,2,1,0:T(8,128)}, u32[]{:S(2)}) copy-start(f32[1,1,1,128,128]{4,3,2,1,0:T(8,128)} %param.18) | copy-start | bytes 196612
  52.0 5.3 %copy-start.8 = (f32[515,128]{1,0:T(8,128)}, f32[515,128]{1,0:T(8,128)S(1)}, u32[]{:S(2)}) copy-start(f32[515,128]{1,0:T(8,128)S(1)} %convolution_add_fusion.2) | copy-start | bytes 791044
  52.7 1.3 %copy-start.5 = (f32[128,1792]{1,0:T(8,128)S(1)}, f32[128,1792]{1,0:T(8,128)}, u32[]{:S(2)}) copy-start(f32[128,1792]{1,0:T(8,128)} %copy-done.4) | copy-start | bytes 2752516
  53.4 4.9 %copy-start.9 = (f32[515,128]{1,0:T(8,128)}, f32[515,128]{1,0:T(8,128)S(1)}, u32[]{:S(2)}) copy-start(f32[515,128]{1,0:T(8,128)S(1)} %convolution_add_fusion.1) | copy-start | bytes 791044
  54.1 5.3 %copy-start.12 = (f32[128,1792]{1,0:T(8,128)S(1)}, f32[128,1792]{1,0:T(8,128)}, u32[]{:S(2)}) copy-start(f32[128,1792]{1,0:T(8,128)} %copy-done.11) | copy-start | bytes 2752516
  54.1 5.3 %copy-start.14 = (f32[128,1792]{1,0:T(8,128)S(1)}, f32[128,1792]{1,0:T(8,128)}, u32[]{:S(2)}) copy-start(f32[128,1792]{1,0:T(8,128)} %copy-done.13) | copy-start | bytes 2752516
  54.1 5.3 %copy-start.26 = (f32[128,1792]{1,0:T(8,128)S(1)}, f32[128,1792]{1,0:T(8,128)}, u32[]{:S(2)}) copy-start(f32[128,1792]{1,0:T(8,128)} %copy-done.25) | copy-start | bytes 2752516
  55.3 44.4 %collective-permute-start.5 = (f32[516,128]{1,0:T(8,128)S(1)}, f32[516,128]{1,0:T(8,128)S(1)}, u32[]{:S(2)}, u32[]{:S(2)}) collective-permute-start(f32[516,128]{1,0:T(8,128)S(1)} %pad_maximum_fusion.13), channel_id=1, source_target_pairs={{7,0},{0,1},{1,2},{2,3},{3,4},{4,5},{5,6},{6,7},{15,8},{8,9},{9,10... | collective-permute-start | bytes 792584 | tf_op jit(solution)/shard_map/ppermute | solution.py:15
  59.4 1.2 copy-start.3
  60.6 5.4 %slice-start.1 = ((f32[515,128]{1,0:T(8,128)}), f32[387,128]{1,0:T(8,128)S(1)}, s32[]{:S(2)}) async-start(f32[515,128]{1,0:T(8,128)} %copy-done.9), calls=%async_computation.1 | async-start | bytes 401408 | tf_op jit(solution)/shard_map/transpose(jvp())/split | solution.py:197
  61.4 13.1 %slice-start = ((f32[515,128]{1,0:T(8,128)}), f32[387,128]{1,0:T(8,128)S(1)}, s32[]{:S(2)}) async-start(f32[515,128]{1,0:T(8,128)} %copy-done.8), calls=%async_computation | async-start | bytes 401408 | tf_op jit(solution)/shard_map/transpose(jvp())/split | solution.py:197
  61.5 3.3 %collective-permute-start.6 = (f32[400,128]{1,0:T(8,128)S(1)}, f32[400,128]{1,0:T(8,128)S(1)}, u32[]{:S(2)}, u32[]{:S(2)}) collective-permute-start(f32[400,128]{1,0:T(8,128)S(1)} %slice_select_fusion), channel_id=1, source_target_pairs={{0,32},{32,0},{64,96},{96,64},{128,160},{160,128},{192,224},{224,1... | collective-permute-start | bytes 614408 | tf_op jit(solution)/shard_map/ppermute | solution.py:93
  64.9 5.4 %collective-permute-start.7 = (f32[200,128]{1,0:T(8,128)S(1)}, f32[200,128]{1,0:T(8,128)S(1)}, u32[]{:S(2)}, u32[]{:S(2)}) collective-permute-start(f32[200,128]{1,0:T(8,128)S(1)} %slice_select_fusion.1), channel_id=1, source_target_pairs={{0,192},{32,224},{64,128},{96,160},{128,64},{160,96},{192,0},{224,... | collective-permute-start | bytes 307208 | tf_op jit(solution)/shard_map/ppermute | solution.py:93
  70.3 3.1 %collective-permute-start.8 = (f32[100,128]{1,0:T(8,128)S(1)}, f32[100,128]{1,0:T(8,128)S(1)}, u32[]{:S(2)}, u32[]{:S(2)}) collective-permute-start(f32[100,128]{1,0:T(8,128)S(1)} %slice_select_fusion.2), channel_id=1, source_target_pairs={{0,64},{32,96},{64,0},{96,32},{128,192},{160,224},{192,128},{224,1... | collective-permute-start | bytes 153608 | tf_op jit(solution)/shard_map/ppermute | solution.py:93
  70.5 35.0 %copy-start.24 = (f32[8]{0:T(128)S(1)}, f32[8]{0:T(128)}, u32[]{:S(2)}) copy-start(f32[8]{0:T(128)} %param.35) | copy-start | bytes 100
  70.5 29.3 %collective-permute-start.4 = (f32[516,128]{1,0:T(8,128)S(1)}, f32[516,128]{1,0:T(8,128)S(1)}, u32[]{:S(2)}, u32[]{:S(2)}) collective-permute-start(f32[516,128]{1,0:T(8,128)S(1)} %pad_maximum_fusion.12), channel_id=1, source_target_pairs={{24,0},{0,8},{8,16},{16,24},{25,1},{1,9},{9,17},{17,25},{26,2},{2,... | collective-permute-start | bytes 792584 | tf_op jit(solution)/shard_map/ppermute | solution.py:15
  73.4 7.4 %collective-permute-start.9 = (f32[100,128]{1,0:T(8,128)S(1)}, f32[100,128]{1,0:T(8,128)S(1)}, u32[]{:S(2)}, u32[]{:S(2)}) collective-permute-start(f32[100,128]{1,0:T(8,128)S(1)} %select_add_fusion.2), channel_id=1, source_target_pairs={{0,1},{1,0},{2,3},{3,2},{4,5},{5,4},{6,7},{7,6},{8,9},{9,8},{10,11... | collective-permute-start | bytes 153608 | tf_op jit(solution)/shard_map/ppermute | solution.py:95
  80.8 5.6 %collective-permute-start.10 = (f32[100,128]{1,0:T(8,128)S(1)}, f32[100,128]{1,0:T(8,128)S(1)}, u32[]{:S(2)}, u32[]{:S(2)}) collective-permute-start(f32[100,128]{1,0:T(8,128)S(1)} %add.209), channel_id=1, source_target_pairs={{0,2},{1,3},{2,0},{3,1},{4,6},{5,7},{6,4},{7,5},{8,10},{9,11},{10,... | collective-permute-start | bytes 153608 | tf_op jit(solution)/shard_map/ppermute | solution.py:95
  80.9 18.8 %collective-permute-start.3 = (f32[516,128]{1,0:T(8,128)S(1)}, f32[516,128]{1,0:T(8,128)S(1)}, u32[]{:S(2)}, u32[]{:S(2)}) collective-permute-start(f32[516,128]{1,0:T(8,128)S(1)} %pad_maximum_fusion.11), channel_id=1, source_target_pairs={{224,0},{0,32},{32,64},{64,96},{96,128},{128,160},{160,192},{192,2... | collective-permute-start | bytes 792584 | tf_op jit(solution)/shard_map/ppermute | solution.py:15
  86.4 4.6 %collective-permute-start.11 = (f32[100,128]{1,0:T(8,128)S(1)}, f32[100,128]{1,0:T(8,128)S(1)}, u32[]{:S(2)}, u32[]{:S(2)}) collective-permute-start(f32[100,128]{1,0:T(8,128)S(1)} %add.210), channel_id=1, source_target_pairs={{0,6},{1,7},{2,4},{3,5},{4,2},{5,3},{6,0},{7,1},{8,14},{9,15},{10,... | collective-permute-start | bytes 153608 | tf_op jit(solution)/shard_map/ppermute | solution.py:95
  91.0 4.0 %collective-permute-start.12 = (f32[100,128]{1,0:T(8,128)S(1)}, f32[100,128]{1,0:T(8,128)S(1)}, u32[]{:S(2)}, u32[]{:S(2)}) collective-permute-start(f32[100,128]{1,0:T(8,128)S(1)} %add.211), channel_id=1, source_target_pairs={{0,8},{8,0},{16,24},{24,16},{1,9},{9,1},{17,25},{25,17},{2,10},{10... | collective-permute-start | bytes 153608 | tf_op jit(solution)/shard_map/ppermute | solution.py:95
  95.0 6.3 %collective-permute-start.13 = (f32[100,128]{1,0:T(8,128)S(1)}, f32[100,128]{1,0:T(8,128)S(1)}, u32[]{:S(2)}, u32[]{:S(2)}) collective-permute-start(f32[100,128]{1,0:T(8,128)S(1)} %add.212), channel_id=1, source_target_pairs={{0,24},{8,16},{16,8},{24,0},{1,25},{9,17},{17,9},{25,1},{2,26},{10... | collective-permute-start | bytes 153608 | tf_op jit(solution)/shard_map/ppermute | solution.py:95
  101.3 3.4 %collective-permute-start.14 = (f32[100,128]{1,0:T(8,128)S(1)}, f32[100,128]{1,0:T(8,128)S(1)}, u32[]{:S(2)}, u32[]{:S(2)}) collective-permute-start(f32[100,128]{1,0:T(8,128)S(1)} %add.213), channel_id=1, source_target_pairs={{0,64},{32,96},{64,0},{96,32},{128,192},{160,224},{192,128},{224,1... | collective-permute-start | bytes 153608 | tf_op jit(solution)/shard_map/ppermute | solution.py:98
  104.7 4.8 %collective-permute-start.15 = (f32[200,128]{1,0:T(8,128)S(1)}, f32[200,128]{1,0:T(8,128)S(1)}, u32[]{:S(2)}, u32[]{:S(2)}) collective-permute-start(f32[200,128]{1,0:T(8,128)S(1)} %maximum_select_fusion.1), channel_id=1, source_target_pairs={{0,192},{32,224},{64,128},{96,160},{128,64},{160,96},{192,0},{224,... | collective-permute-start | bytes 307208 | tf_op jit(solution)/shard_map/ppermute | solution.py:98
  109.5 7.8 %collective-permute-start.16 = (f32[400,128]{1,0:T(8,128)S(1)}, f32[400,128]{1,0:T(8,128)S(1)}, u32[]{:S(2)}, u32[]{:S(2)}) collective-permute-start(f32[400,128]{1,0:T(8,128)S(1)} %maximum_select_fusion), channel_id=1, source_target_pairs={{0,32},{32,0},{64,96},{96,64},{128,160},{160,128},{192,224},{224,1... | collective-permute-start | bytes 614408 | tf_op jit(solution)/shard_map/ppermute | solution.py:98
